TPU v7x, 256 devices: a whole 4x4x8 slice. The times are simulated.
256 devices in a mesh: pipe: 2 (over core), seq: 32 (over x, z), chan: 4 (over y).
Axes of the slice: x: 4, y: 4, z: 8, core: 2. Of those that a mesh axis runs over, the one named last changes fastest.
Arguments:
- grad_out: bfloat16 [2, 8192, 2048], P('pipe', 'seq', 'chan'), may hold values from -6 to 6
- value_branch: bfloat16 [2, 8192, 2048], P('pipe', 'seq', 'chan'), may hold values from -0.0625 to 0.0625
- key_gate: bfloat16 [2, 8192, 2048], P('pipe', 'seq', 'chan'), may hold values from -6 to 6
- query_gate: bfloat16 [2, 8192, 2048], P('pipe', 'seq', 'chan'), may hold values from -6 to 6
- short_weights: float32 [2, 3, 2048], P('pipe', None, 'chan'), may hold values from -3 to 3
- long_filters: bfloat16 [2, 8192, 2048], P('pipe', 'seq', 'chan'), may hold values from -0.0625 to 0.0625
Outputs:
- passed_grad: bfloat16 [2, 8192, 2048], P('pipe', 'seq', 'chan')
- filter_grad: float32 [2, 8192, 2048], P('pipe', 'seq', 'chan')
All inputs are finite; a program needn't handle non-finite values.
Results may differ from a plain program's by a relative error of at most 0.0049.
Values may be sent and summed in bfloat16 or wider, within the bound.
No kernel may reach another device: no remote copies, remote signals or barrier semaphores. Data moves between devices by JAX's collectives and lax.ppermute only.
A program may use at most 64 MiB of HBM per device.

v0:
```python
import math

import numpy as np

import jax
import jax.numpy as jnp
from jax import lax
from jax.sharding import PartitionSpec as P

PRECISION = lax.Precision.HIGHEST


def shifted(block, axis, distance):
    devices = range(lax.axis_size(axis))
    route = [((i - distance) % len(devices), i) for i in devices]
    return lax.ppermute(block, axis, route)


def angle_table(first, second, modulus):
    angles = (np.outer(first, second) % modulus) * (2.0 * math.pi / modulus)
    return np.cos(angles), np.sin(angles)


def contract(form, table, values):
    return jnp.einsum(form, jnp.asarray(table, jnp.float32), values, precision=PRECISION)


def forward(signal, padded):
    blocks, _, rows = signal.shape
    half = np.arange(blocks + 1)
    cos_b, sin_b = angle_table(half, np.arange(blocks), 2 * blocks)
    real = contract("ca,akr->ckr", cos_b, signal)
    imag = -contract("ca,akr->ckr", sin_b, signal)
    cos_t, sin_t = angle_table(half, np.arange(rows), padded)
    cos_t = jnp.asarray(cos_t, jnp.float32)[:, None, :]
    sin_t = jnp.asarray(sin_t, jnp.float32)[:, None, :]
    twisted_real = real * cos_t + imag * sin_t
    twisted_imag = imag * cos_t - real * sin_t
    cos_r, sin_r = angle_table(np.arange(rows), np.arange(rows), rows)
    out_real = jnp.einsum("ckr,rd->ckd", twisted_real, jnp.asarray(cos_r, jnp.float32), precision=PRECISION) + jnp.einsum(
        "ckr,rd->ckd", twisted_imag, jnp.asarray(sin_r, jnp.float32), precision=PRECISION
    )
    out_imag = jnp.einsum("ckr,rd->ckd", twisted_imag, jnp.asarray(cos_r, jnp.float32), precision=PRECISION) - jnp.einsum(
        "ckr,rd->ckd", twisted_real, jnp.asarray(sin_r, jnp.float32), precision=PRECISION
    )
    return out_real, out_imag


def inverse(real, imag, padded):
    half_count, _, rows = real.shape
    blocks = half_count - 1
    half = np.arange(half_count)
    cos_r, sin_r = angle_table(np.arange(rows), np.arange(rows), rows)
    cos_r = jnp.asarray(cos_r, jnp.float32)
    sin_r = jnp.asarray(sin_r, jnp.float32)
    back_real = jnp.einsum("ckd,dr->ckr", real, cos_r, precision=PRECISION) - jnp.einsum(
        "ckd,dr->ckr", imag, sin_r, precision=PRECISION
    )
    back_imag = jnp.einsum("ckd,dr->ckr", imag, cos_r, precision=PRECISION) + jnp.einsum(
        "ckd,dr->ckr", real, sin_r, precision=PRECISION
    )
    cos_t, sin_t = angle_table(half, np.arange(rows), padded)
    cos_t = jnp.asarray(cos_t, jnp.float32)[:, None, :]
    sin_t = jnp.asarray(sin_t, jnp.float32)[:, None, :]
    twisted_real = back_real * cos_t - back_imag * sin_t
    twisted_imag = back_imag * cos_t + back_real * sin_t
    weight = np.full(half_count, 2.0)
    weight[0] = 1.0
    weight[blocks] = 1.0
    cos_b, sin_b = angle_table(np.arange(blocks), half, 2 * blocks)
    cos_b = cos_b * weight[None, :] / padded
    sin_b = sin_b * weight[None, :] / padded
    return contract("ac,ckr->akr", cos_b, twisted_real) - contract("ac,ckr->akr", sin_b, twisted_imag)


def body(grad_out, value_branch, key_gate, query_gate, short_weights, long_filters):
    rows, columns = grad_out.shape[1:]
    devices = lax.axis_size("seq")
    position = lax.axis_index("seq")
    group = columns // devices
    padded = 2 * rows * devices
    grad_conv = (query_gate[0].astype(jnp.float32) * grad_out[0].astype(jnp.float32)).astype(jnp.bfloat16)
    gated_value = (key_gate[0].astype(jnp.float32) * value_branch[0].astype(jnp.float32)).astype(jnp.bfloat16)
    stacked = jnp.stack([grad_conv, gated_value, long_filters[0], key_gate[0]])
    send = jnp.swapaxes(stacked, 1, 2).reshape(4, devices, group, rows)
    recv = lax.all_to_all(send, "seq", split_axis=1, concat_axis=1, tiled=True)
    conv_real, conv_imag = forward(recv[0].astype(jnp.float32), padded)
    gated_real, gated_imag = forward(recv[1].astype(jnp.float32), padded)
    filter_real, filter_imag = forward(recv[2].astype(jnp.float32), padded)
    back_real = conv_real * filter_real + conv_imag * filter_imag
    back_imag = conv_imag * filter_real - conv_real * filter_imag
    fold_real = conv_real * gated_real + conv_imag * gated_imag
    fold_imag = conv_imag * gated_real - conv_real * gated_imag
    grad_gated = inverse(back_real, back_imag, padded)
    grad_filter = inverse(fold_real, fold_imag, padded)
    grad_value = recv[3].astype(jnp.float32) * grad_gated
    rim = jnp.concatenate(
        [grad_value[1:, :, :2], jnp.zeros((1, group, 2), grad_value.dtype)], axis=0
    )
    longer = jnp.concatenate([grad_value, rim], axis=2)
    weights = lax.dynamic_slice_in_dim(short_weights[0], position * group, group, axis=1)
    weights = weights[:, None, :, None]
    grad_input = (
        weights[0] * longer[:, :, :rows]
        + weights[1] * longer[:, :, 1 : rows + 1]
        + weights[2] * longer[:, :, 2:]
    ).astype(jnp.bfloat16)
    input_back = lax.all_to_all(grad_input, "seq", split_axis=0, concat_axis=0, tiled=True)
    filter_back = lax.all_to_all(grad_filter, "seq", split_axis=0, concat_axis=0, tiled=True)
    input_tokens = input_back.reshape(columns, rows).T
    filter_tokens = filter_back.reshape(columns, rows).T
    passed = shifted(input_tokens[None], "pipe", -1)
    return (passed, filter_tokens[None])


def solution(mesh):
    placed = (
        P("pipe", "seq", "chan"),
        P("pipe", "seq", "chan"),
        P("pipe", "seq", "chan"),
        P("pipe", "seq", "chan"),
        P("pipe", None, "chan"),
        P("pipe", "seq", "chan"),
    )
    return jax.shard_map(
        body,
        mesh=mesh,
        in_specs=placed,
        out_specs=(P("pipe", "seq", "chan"), P("pipe", "seq", "chan")),
        check_vma=False,
    )
```

profile of v0, /device:TPU:48, one launch (start us, length us, event | category | flops | bytes accessed | tf_op | source)
XLA Modules:
  0.0 108.7 jit_solution(7747975102143963510)
XLA Ops:
  0.6 1.1 %copy.97 = bf16[1,256,512]{1,2,0:T(8,128)(2,1)S(1)} copy(bf16[1,256,512]{2,1,0:T(8,128)(2,1)} %param.44) | data formatting | bytes 524288 | tf_op args[2]
  3.8 0.8 copy-done.7
  5.0 1.1 %copy.101 = bf16[4,32,16,256]{3,2,0,1:T(8,128)(2,1)} copy(bf16[4,32,16,256]{3,2,1,0:T(8,128)(2,1)S(1)} %bitcast.86) | data formatting | bytes 2097152 | tf_op jit(solution)/shard_map/reshape | solution.py:85
  6.2 11.2 %all-to-all-start = ((bf16[4,32,16,256]{3,2,0,1:T(8,128)(2,1)}), bf16[4,32,16,256]{3,2,0,1:T(8,128)(2,1)S(1)}, u32[]{:S(2)}, u32[]{:S(2)}) async-start(bf16[4,32,16,256]{3,2,0,1:T(8,128)(2,1)} %copy.101), calls=%async_computation | async-start | bytes 2097152 | tf_op jit(solution)/shard_map/all_to_all | solution.py:86
  18.2 27.7 %all-to-all-done = bf16[4,32,16,256]{3,2,0,1:T(8,128)(2,1)S(1)} async-done(((bf16[4,32,16,256]{3,2,0,1:T(8,128)(2,1)}), bf16[4,32,16,256]{3,2,0,1:T(8,128)(2,1)S(1)}, u32[]{:S(2)}, u32[]{:S(2)}) %all-to-all-start) | async-done | bytes 1048608 | tf_op jit(solution)/shard_map/all_to_all | solution.py:86
  48.9 1.0 multiply_add_fusion
  58.0 0.9 multiply_add_fusion.3
  58.9 1.1 %fusion.10 = f32[33,16,256]{2,0,1:T(8,128)S(1)} fusion(f32[256,256,1]{1,0,2:T(8,128)S(1)} %copy-done.1, f32[33,16,256]{2,1,0:T(8,128)S(1)} %get-tuple-element.6), kind=kOutput, calls=%fused_computation.28 | convolution fusion | flops 415236096 | bytes 1343488 | tf_op jit(solution)/shard_map/ckd,dr->ckr/dot_general | solution.py:56
  60.0 0.9 fusion.6
  61.0 0.9 convolution_subtract_fusion
  61.9 0.9 convolution_add_fusion
  62.8 0.9 fusion.12
  63.8 0.9 fusion.16
  64.7 0.9 convolution_add_fusion.1
  65.6 0.9 convolution_subtract_fusion.1
  68.6 0.9 copy.117
  69.5 5.2 %all-to-all-start.1 = ((bf16[32,16,256]{2,1,0:T(8,128)(2,1)}), bf16[32,16,256]{2,1,0:T(8,128)(2,1)S(1)}, u32[]{:S(2)}, u32[]{:S(2)}) async-start(bf16[32,16,256]{2,1,0:T(8,128)(2,1)} %copy.117), calls=%async_computation.1 | async-start | bytes 524288 | tf_op jit(solution)/shard_map/all_to_all | solution.py:108
  76.1 1.1 %copy.127 = f32[32,16,256]{2,1,0:T(8,128)} copy(f32[32,16,256]{2,0,1:T(8,128)S(1)} %fusion.3) | data formatting | bytes 1048576 | tf_op jit(solution)/shard_map/sub | solution.py:73
  77.2 9.2 %all-to-all-done.1 = bf16[32,16,256]{2,1,0:T(8,128)(2,1)S(1)} async-done(((bf16[32,16,256]{2,1,0:T(8,128)(2,1)}), bf16[32,16,256]{2,1,0:T(8,128)(2,1)S(1)}, u32[]{:S(2)}, u32[]{:S(2)}) %all-to-all-start.1) | async-done | bytes 262176 | tf_op jit(solution)/shard_map/all_to_all | solution.py:108
  86.5 4.6 %all-to-all-start.2 = ((f32[32,16,256]{2,1,0:T(8,128)}), f32[32,16,256]{2,1,0:T(8,128)S(1)}, u32[]{:S(2)}, u32[]{:S(2)}) async-start(f32[32,16,256]{2,1,0:T(8,128)} %copy.127), calls=%async_computation.2 | async-start | bytes 1048576 | tf_op jit(solution)/shard_map/all_to_all | solution.py:109
  91.1 1.5 %collective-permute-done = bf16[1,256,512]{1,2,0:T(8,128)(2,1)S(1)} collective-permute-done((bf16[1,256,512]{1,2,0:T(8,128)(2,1)S(1)}, bf16[1,256,512]{1,2,0:T(8,128)(2,1)S(1)}, u32[]{:S(2)}, u32[]{:S(2)}) %collective-permute-start) | collective-permute-done | bytes 262176 | tf_op jit(solution)/shard_map/ppermute | solution.py:16
  92.7 0.8 copy.128
  93.5 14.2 %all-to-all-done.2 = f32[32,16,256]{2,1,0:T(8,128)S(1)} async-done(((f32[32,16,256]{2,1,0:T(8,128)}), f32[32,16,256]{2,1,0:T(8,128)S(1)}, u32[]{:S(2)}, u32[]{:S(2)}) %all-to-all-start.2) | async-done | bytes 524320 | tf_op jit(solution)/shard_map/all_to_all | solution.py:109
  107.7 1.0 copy.129
  (55 shorter events, 17.6 us)
Async XLA Ops:
  0.6 1.1 %copy-start.4 = (bf16[1,256,512]{2,1,0:T(8,128)(2,1)S(1)}, bf16[1,256,512]{2,1,0:T(8,128)(2,1)}, u32[]{:S(2)}) copy-start(bf16[1,256,512]{2,1,0:T(8,128)(2,1)} %param.42) | copy-start | bytes 786436
  1.8 1.0 copy-start.5
  2.7 0.9 copy-start.6
  3.7 0.9 copy-start.7
  6.2 39.7 %all-to-all-start = ((bf16[4,32,16,256]{3,2,0,1:T(8,128)(2,1)}), bf16[4,32,16,256]{3,2,0,1:T(8,128)(2,1)S(1)}, u32[]{:S(2)}, u32[]{:S(2)}) async-start(bf16[4,32,16,256]{3,2,0,1:T(8,128)(2,1)} %copy.101), calls=%async_computation | async-start | bytes 2097152 | tf_op jit(solution)/shard_map/all_to_all | solution.py:86
  18.2 27.8 %copy-start.9 = (f32[33,32,1]{0,1,2:T(8,128)S(1)}, f32[33,32,1]{0,1,2:T(8,128)}, u32[]{:S(2)}) copy-start(f32[33,32,1]{0,1,2:T(8,128)} %constant.48) | copy-start | bytes 12676
  46.0 0.7 copy-start.8
  48.1 0.8 copy-start.2
  48.1 0.8 copy-start.3
  48.9 1.0 copy-start.1
  50.7 1.0 copy-start
  65.6 0.9 copy-start.11
  66.6 0.7 copy-start.10
  69.5 17.0 %all-to-all-start.1 = ((bf16[32,16,256]{2,1,0:T(8,128)(2,1)}), bf16[32,16,256]{2,1,0:T(8,128)(2,1)S(1)}, u32[]{:S(2)}, u32[]{:S(2)}) async-start(bf16[32,16,256]{2,1,0:T(8,128)(2,1)} %copy.117), calls=%async_computation.1 | async-start | bytes 524288 | tf_op jit(solution)/shard_map/all_to_all | solution.py:108
  86.5 21.2 %all-to-all-start.2 = ((f32[32,16,256]{2,1,0:T(8,128)}), f32[32,16,256]{2,1,0:T(8,128)S(1)}, u32[]{:S(2)}, u32[]{:S(2)}) async-start(f32[32,16,256]{2,1,0:T(8,128)} %copy.127), calls=%async_computation.2 | async-start | bytes 1048576 | tf_op jit(solution)/shard_map/all_to_all | solution.py:109
  91.0 1.6 %collective-permute-start = (bf16[1,256,512]{1,2,0:T(8,128)(2,1)S(1)}, bf16[1,256,512]{1,2,0:T(8,128)(2,1)S(1)}, u32[]{:S(2)}, u32[]{:S(2)}) collective-permute-start(bf16[1,256,512]{1,2,0:T(8,128)(2,1)S(1)} %bitcast.88), channel_id=1, source_target_pairs={{128,0},{0,128},{129,1},{1,129},{130,2},{2,130},{131,3},{3,131},{1... | collective-permute-start | bytes 786440 | tf_op jit(solution)/shard_map/ppermute | solution.py:16
where the time goes:
time: 109 us
  waiting for transfers between devices  52.7 us (48%)
  matrix products  22.4 us (21%)
  starting transfers between devices  21 us (19%)
  local copies, waits for them, and re-layouts  10.7 us (10%)
  between operations  1.09 us (1%)
    all_to_all x1, waiting for transfers between devices, body(): recv = lax.all_to_all(send, 'seq', split_axis=1, concat_axis=1, tiled=True)  27.7 us
    all_to_all x1, waiting for transfers between devices, body(): lax.all_to_all(grad_filter, 'seq', split_axis=0, concat_axis=0, tiled=True)  14.2 us
    all_to_all x1, starting transfers between devices, body(): recv = lax.all_to_all(send, 'seq', split_axis=1, concat_axis=1, tiled=True)  11.2 us
    all_to_all x1, waiting for transfers between devices, body(): lax.all_to_all(grad_input, 'seq', split_axis=0, concat_axis=0, tiled=True)  9.25 us
    unnamed x31, local copies, waits for them, and re-layouts  6.73 us
    dot_general x10, matrix products, contract(): jnp.einsum(form, jnp.asarray(table, jnp.float32), values, precision=PRECI...  6.25 us
    all_to_all x1, starting transfers between devices, body(): lax.all_to_all(grad_input, 'seq', split_axis=0, concat_axis=0, tiled=True)  5.19 us
    all_to_all x1, starting transfers between devices, body(): lax.all_to_all(grad_filter, 'seq', split_axis=0, concat_axis=0, tiled=True)  4.56 us
  transfers between devices with their start and end apart: 4, of which 4 were waited for; matrix products, arithmetic and copies ran while one was open for 4% of the time, Pallas kernels for 0%

commit v1 on v0

--- a/solution.py
+++ b/solution.py
@@ -105,9 +105,14 @@
         + weights[1] * longer[:, :, 1 : rows + 1]
         + weights[2] * longer[:, :, 2:]
     ).astype(jnp.bfloat16)
-    input_back = lax.all_to_all(grad_input, "seq", split_axis=0, concat_axis=0, tiled=True)
-    filter_back = lax.all_to_all(grad_filter, "seq", split_axis=0, concat_axis=0, tiled=True)
-    input_tokens = input_back.reshape(columns, rows).T
+    filter_high = lax.reduce_precision(grad_filter, exponent_bits=8, mantissa_bits=7)
+    filter_low = grad_filter - filter_high
+    outgoing = jnp.stack(
+        [grad_input, filter_high.astype(jnp.bfloat16), filter_low.astype(jnp.bfloat16)]
+    )
+    returned = lax.all_to_all(outgoing, "seq", split_axis=1, concat_axis=1, tiled=True)
+    input_tokens = returned[0].reshape(columns, rows).T
+    filter_back = returned[1].astype(jnp.float32) + returned[2].astype(jnp.float32)
     filter_tokens = filter_back.reshape(columns, rows).T
     passed = shifted(input_tokens[None], "pipe", -1)
     return (passed, filter_tokens[None])

time: 109 us -> 103 us (0.945)
  the two profiles are of different devices: /device:TPU:48 before, /device:TPU:1 now
where the time goes in v1:
time: 103 us; the launch traced here: 102 us
  blocking collectives  27.9 us (27%)
  waiting for transfers between devices  24.2 us (23%)
  matrix products  22.4 us (22%)
  starting transfers between devices  16.4 us (16%)
  local copies, waits for them, and re-layouts  9.18 us (9%)
  between operations  1.09 us (1%)
    all_to_all x1, blocking collectives, body(): lax.all_to_all(outgoing, 'seq', split_axis=1, concat_axis=1, tiled=True)  27.9 us
    all_to_all x1, waiting for transfers between devices, body(): recv = lax.all_to_all(send, 'seq', split_axis=1, concat_axis=1, tiled=True)  24.1 us
    all_to_all x1, starting transfers between devices, body(): recv = lax.all_to_all(send, 'seq', split_axis=1, concat_axis=1, tiled=True)  11.9 us
    unnamed x31, local copies, waits for them, and re-layouts  6.73 us
    dot_general x10, matrix products, contract(): jnp.einsum(form, jnp.asarray(table, jnp.float32), values, precision=PRECI...  6.25 us
    ppermute x1, starting transfers between devices, shifted(): return lax.ppermute(block, axis, route)  4.59 us
    dot_general x3, matrix products, forward(): jnp.einsum('ckr,rd->ckd', twisted_real, jnp.asarray(sin_r, jnp.float32),...  2.33 us
    dot_general x3, matrix products, forward(): jnp.einsum('ckr,rd->ckd', twisted_imag, jnp.asarray(sin_r, jnp.float32),...  2.09 us
  transfers between devices with their start and end apart: 2, of which 2 were waited for; matrix products, arithmetic and copies ran while one was open for 2% of the time, Pallas kernels for 0%

profile of v1, /device:TPU:1, one launch (start us, length us, event | category | flops | bytes accessed | tf_op | source)
XLA Modules:
  0.0 102.2 jit_solution(10967921381598253146)
XLA Ops:
  0.6 1.1 %copy.97 = bf16[1,256,512]{1,2,0:T(8,128)(2,1)S(1)} copy(bf16[1,256,512]{2,1,0:T(8,128)(2,1)} %param.44) | data formatting | bytes 524288 | tf_op args[2]
  1.9 0.8 copy-done.5
  2.9 0.8 copy-done.6
  3.8 0.8 copy-done.7
  5.0 1.1 %copy.101 = bf16[4,32,16,256]{3,2,0,1:T(8,128)(2,1)} copy(bf16[4,32,16,256]{3,2,1,0:T(8,128)(2,1)S(1)} %bitcast.104) | data formatting | bytes 2097152 | tf_op jit(solution)/shard_map/reshape | solution.py:85
  6.2 11.9 %all-to-all-start = ((bf16[4,32,16,256]{3,2,0,1:T(8,128)(2,1)}), bf16[4,32,16,256]{3,2,0,1:T(8,128)(2,1)S(1)}, u32[]{:S(2)}, u32[]{:S(2)}) async-start(bf16[4,32,16,256]{3,2,0,1:T(8,128)(2,1)} %copy.101), calls=%async_computation | async-start | bytes 2097152 | tf_op jit(solution)/shard_map/all_to_all | solution.py:86
  18.0 0.8 fusion.69
  18.8 24.1 %all-to-all-done = bf16[4,32,16,256]{3,2,0,1:T(8,128)(2,1)S(1)} async-done(((bf16[4,32,16,256]{3,2,0,1:T(8,128)(2,1)}), bf16[4,32,16,256]{3,2,0,1:T(8,128)(2,1)S(1)}, u32[]{:S(2)}, u32[]{:S(2)}) %all-to-all-start) | async-done | bytes 1048608 | tf_op jit(solution)/shard_map/all_to_all | solution.py:86
  46.0 1.0 multiply_add_fusion.1
  55.0 0.9 multiply_add_fusion.4
  55.9 1.1 %fusion.16 = f32[33,16,256]{2,0,1:T(8,128)S(1)} fusion(f32[256,256,1]{1,0,2:T(8,128)S(1)} %copy-done.1, f32[33,16,256]{2,1,0:T(8,128)S(1)} %get-tuple-element.6), kind=kOutput, calls=%fused_computation.37 | convolution fusion | flops 415236096 | bytes 1343488 | tf_op jit(solution)/shard_map/ckd,dr->ckr/dot_general | solution.py:56
  57.1 0.9 fusion.12
  58.0 0.9 convolution_subtract_fusion.1
  58.9 0.9 convolution_add_fusion.1
  60.6 0.8 fusion.5
  61.5 0.9 fusion.6
  62.4 0.9 fusion.10
  63.3 0.9 convolution_add_fusion
  64.3 0.9 convolution_subtract_fusion
  65.9 0.7 fusion.64
  67.6 27.9 %all_to_all.10 = bf16[3,32,16,256]{3,2,0,1:T(8,128)(2,1)S(1)} all-to-all(bf16[3,32,16,256]{3,2,0,1:T(8,128)(2,1)S(1)} %copy.126), channel_id=1, replica_groups=mesh['pipe'=2,'seq'=32,'chan'=4] {'seq'}, dimensions={1} | all-to-all | bytes 1572864 | tf_op jit(solution)/shard_map/all_to_all | solution.py:113
  95.6 4.6 %collective-permute-start = (bf16[1,256,512]{1,2,0:T(8,128)(2,1)S(1)}, bf16[1,256,512]{1,2,0:T(8,128)(2,1)S(1)}, u32[]{:S(2)}, u32[]{:S(2)}) collective-permute-start(bf16[1,256,512]{1,2,0:T(8,128)(2,1)S(1)} %bitcast.106), channel_id=1, source_target_pairs={{128,0},{0,128},{129,1},{1,129},{130,2},{2,130},{131,3},{3,131},{1... | collective-permute-start | bytes 786440 | tf_op jit(solution)/shard_map/ppermute | solution.py:16
  100.2 1.0 copy.131
  101.3 0.8 copy.130
  (54 shorter events, 14.3 us)
Async XLA Ops:
  0.6 1.1 %copy-start.4 = (bf16[1,256,512]{2,1,0:T(8,128)(2,1)S(1)}, bf16[1,256,512]{2,1,0:T(8,128)(2,1)}, u32[]{:S(2)}) copy-start(bf16[1,256,512]{2,1,0:T(8,128)(2,1)} %param.42) | copy-start | bytes 786436
  1.8 1.0 copy-start.5
  2.7 0.9 copy-start.6
  3.7 0.9 copy-start.7
  6.2 36.7 %all-to-all-start = ((bf16[4,32,16,256]{3,2,0,1:T(8,128)(2,1)}), bf16[4,32,16,256]{3,2,0,1:T(8,128)(2,1)S(1)}, u32[]{:S(2)}, u32[]{:S(2)}) async-start(bf16[4,32,16,256]{3,2,0,1:T(8,128)(2,1)} %copy.101), calls=%async_computation | async-start | bytes 2097152 | tf_op jit(solution)/shard_map/all_to_all | solution.py:86
  18.8 24.2 %copy-start.9 = (f32[33,32,1]{0,1,2:T(8,128)S(1)}, f32[33,32,1]{0,1,2:T(8,128)}, u32[]{:S(2)}) copy-start(f32[33,32,1]{0,1,2:T(8,128)} %constant.48) | copy-start | bytes 12676
  43.0 0.7 copy-start.8
  45.1 0.8 copy-start.2
  45.2 0.8 copy-start.3
  46.0 1.0 copy-start.1
  47.7 1.0 copy-start
  58.9 0.9 copy-start.11
  59.9 0.7 copy-start.10
  95.6 5.8 %collective-permute-start = (bf16[1,256,512]{1,2,0:T(8,128)(2,1)S(1)}, bf16[1,256,512]{1,2,0:T(8,128)(2,1)S(1)}, u32[]{:S(2)}, u32[]{:S(2)}) collective-permute-start(bf16[1,256,512]{1,2,0:T(8,128)(2,1)S(1)} %bitcast.106), channel_id=1, source_target_pairs={{128,0},{0,128},{129,1},{1,129},{130,2},{2,130},{131,3},{3,131},{1... | collective-permute-start | bytes 786440 | tf_op jit(solution)/shard_map/ppermute | solution.py:16

commit v2 on v1

--- a/solution.py
+++ b/solution.py
@@ -7,7 +7,7 @@
 from jax import lax
 from jax.sharding import PartitionSpec as P
 
-PRECISION = lax.Precision.HIGHEST
+PRECISION = lax.Precision.HIGH
 
 
 def shifted(block, axis, distance):

time: 103 us -> 97.5 us (0.947)
  matrix products: 22.4 us -> 16.5 us
    dot_general x10, matrix products: 6.25 us -> 4.6 us  [contract(): jnp.einsum(form, jnp.asarray(table, jnp.float32), values, precision=PRECI...]
where the time goes in v2:
time: 97.5 us; the launch traced here: 96.9 us
  blocking collectives  27.9 us (29%)
  waiting for transfers between devices  24.2 us (25%)
  matrix products  16.5 us (17%)
  starting transfers between devices  16.4 us (17%)
  local copies, waits for them, and re-layouts  9.85 us (10%)
  between operations  1.07 us (1%)
    all_to_all x1, blocking collectives, body(): lax.all_to_all(outgoing, 'seq', split_axis=1, concat_axis=1, tiled=True)  27.9 us
    all_to_all x1, waiting for transfers between devices, body(): recv = lax.all_to_all(send, 'seq', split_axis=1, concat_axis=1, tiled=True)  24.1 us
    all_to_all x1, starting transfers between devices, body(): recv = lax.all_to_all(send, 'seq', split_axis=1, concat_axis=1, tiled=True)  11.9 us
    unnamed x31, local copies, waits for them, and re-layouts  7.4 us
    dot_general x10, matrix products, contract(): jnp.einsum(form, jnp.asarray(table, jnp.float32), values, precision=PRECI...  4.6 us
    ppermute x1, starting transfers between devices, shifted(): return lax.ppermute(block, axis, route)  4.59 us
  transfers between devices with their start and end apart: 2, of which 2 were waited for; matrix products, arithmetic and copies ran while one was open for 2% of the time, Pallas kernels for 0%

profile of v2, /device:TPU:1, one launch (start us, length us, event | category | flops | bytes accessed | tf_op | source)
XLA Modules:
  0.0 96.9 jit_solution(12341723771257366356)
XLA Ops:
  0.6 1.1 %copy.97 = bf16[1,256,512]{1,2,0:T(8,128)(2,1)S(1)} copy(bf16[1,256,512]{2,1,0:T(8,128)(2,1)} %param.44) | data formatting | bytes 524288 | tf_op args[2]
  1.9 0.8 copy-done.5
  2.9 0.8 copy-done.6
  3.8 0.8 copy-done.7
  5.0 1.1 %copy.101 = bf16[4,32,16,256]{3,2,0,1:T(8,128)(2,1)} copy(bf16[4,32,16,256]{3,2,1,0:T(8,128)(2,1)S(1)} %bitcast.104) | data formatting | bytes 2097152 | tf_op jit(solution)/shard_map/reshape | solution.py:85
  6.2 11.9 %all-to-all-start = ((bf16[4,32,16,256]{3,2,0,1:T(8,128)(2,1)}), bf16[4,32,16,256]{3,2,0,1:T(8,128)(2,1)S(1)}, u32[]{:S(2)}, u32[]{:S(2)}) async-start(bf16[4,32,16,256]{3,2,0,1:T(8,128)(2,1)} %copy.101), calls=%async_computation | async-start | bytes 2097152 | tf_op jit(solution)/shard_map/all_to_all | solution.py:86
  18.0 0.8 fusion.69
  18.8 24.1 %all-to-all-done = bf16[4,32,16,256]{3,2,0,1:T(8,128)(2,1)S(1)} async-done(((bf16[4,32,16,256]{3,2,0,1:T(8,128)(2,1)}), bf16[4,32,16,256]{3,2,0,1:T(8,128)(2,1)S(1)}, u32[]{:S(2)}, u32[]{:S(2)}) %all-to-all-start) | async-done | bytes 1048608 | tf_op jit(solution)/shard_map/all_to_all | solution.py:86
  45.7 0.9 multiply_add_fusion.1
  48.6 0.5 convolution_subtract_fusion.3
  52.2 0.5 convolution_add_fusion.2
  52.8 0.7 multiply_add_fusion.4
  53.5 0.7 fusion.16
  54.2 0.7 fusion.12
  54.9 0.7 convolution_subtract_fusion.1
  55.6 0.7 convolution_add_fusion.1
  57.6 0.8 fusion.6
  58.4 0.7 fusion.10
  59.1 0.7 convolution_add_fusion
  59.8 0.7 convolution_subtract_fusion
  62.3 27.9 %all_to_all.10 = bf16[3,32,16,256]{3,2,0,1:T(8,128)(2,1)S(1)} all-to-all(bf16[3,32,16,256]{3,2,0,1:T(8,128)(2,1)S(1)} %copy.126), channel_id=1, replica_groups=mesh['pipe'=2,'seq'=32,'chan'=4] {'seq'}, dimensions={1} | all-to-all | bytes 1572864 | tf_op jit(solution)/shard_map/all_to_all | solution.py:113
  90.3 4.6 %collective-permute-start = (bf16[1,256,512]{1,2,0:T(8,128)(2,1)S(1)}, bf16[1,256,512]{1,2,0:T(8,128)(2,1)S(1)}, u32[]{:S(2)}, u32[]{:S(2)}) collective-permute-start(bf16[1,256,512]{1,2,0:T(8,128)(2,1)S(1)} %bitcast.106), channel_id=1, source_target_pairs={{128,0},{0,128},{129,1},{1,129},{130,2},{2,130},{131,3},{3,131},{1... | collective-permute-start | bytes 786440 | tf_op jit(solution)/shard_map/ppermute | solution.py:16
  94.9 1.0 %copy.131 = f32[1,256,512]{2,1,0:T(8,128)} copy(f32[1,256,512]{1,2,0:T(8,128)S(1)} %bitcast.105) | data formatting | bytes 1048576
  96.0 0.8 copy.130
  (54 shorter events, 11.8 us)
Async XLA Ops:
  0.6 1.1 %copy-start.4 = (bf16[1,256,512]{2,1,0:T(8,128)(2,1)S(1)}, bf16[1,256,512]{2,1,0:T(8,128)(2,1)}, u32[]{:S(2)}) copy-start(bf16[1,256,512]{2,1,0:T(8,128)(2,1)} %param.42) | copy-start | bytes 786436
  1.8 1.0 copy-start.5
  2.7 0.9 copy-start.6
  3.7 0.9 copy-start.7
  6.2 36.7 %all-to-all-start = ((bf16[4,32,16,256]{3,2,0,1:T(8,128)(2,1)}), bf16[4,32,16,256]{3,2,0,1:T(8,128)(2,1)S(1)}, u32[]{:S(2)}, u32[]{:S(2)}) async-start(bf16[4,32,16,256]{3,2,0,1:T(8,128)(2,1)} %copy.101), calls=%async_computation | async-start | bytes 2097152 | tf_op jit(solution)/shard_map/all_to_all | solution.py:86
  18.8 24.2 %copy-start.9 = (f32[33,32,1]{0,1,2:T(8,128)S(1)}, f32[33,32,1]{0,1,2:T(8,128)}, u32[]{:S(2)}) copy-start(f32[33,32,1]{0,1,2:T(8,128)} %constant.48) | copy-start | bytes 12676
  43.0 0.7 copy-start.8
  44.9 0.8 copy-start.2
  44.9 0.8 copy-start.3
  45.7 0.9 copy-start.1
  47.2 1.0 copy-start
  55.6 0.7 copy-start.11
  56.3 0.7 copy-start.10
  90.3 5.8 %collective-permute-start = (bf16[1,256,512]{1,2,0:T(8,128)(2,1)S(1)}, bf16[1,256,512]{1,2,0:T(8,128)(2,1)S(1)}, u32[]{:S(2)}, u32[]{:S(2)}) collective-permute-start(bf16[1,256,512]{1,2,0:T(8,128)(2,1)S(1)} %bitcast.106), channel_id=1, source_target_pairs={{128,0},{0,128},{129,1},{1,129},{130,2},{2,130},{131,3},{3,131},{1... | collective-permute-start | bytes 786440 | tf_op jit(solution)/shard_map/ppermute | solution.py:16

commit v3 on v2

--- a/solution.py
+++ b/solution.py
@@ -105,14 +105,10 @@
         + weights[1] * longer[:, :, 1 : rows + 1]
         + weights[2] * longer[:, :, 2:]
     ).astype(jnp.bfloat16)
-    filter_high = lax.reduce_precision(grad_filter, exponent_bits=8, mantissa_bits=7)
-    filter_low = grad_filter - filter_high
-    outgoing = jnp.stack(
-        [grad_input, filter_high.astype(jnp.bfloat16), filter_low.astype(jnp.bfloat16)]
-    )
+    outgoing = jnp.stack([grad_input, grad_filter.astype(jnp.bfloat16)])
     returned = lax.all_to_all(outgoing, "seq", split_axis=1, concat_axis=1, tiled=True)
     input_tokens = returned[0].reshape(columns, rows).T
-    filter_back = returned[1].astype(jnp.float32) + returned[2].astype(jnp.float32)
+    filter_back = returned[1].astype(jnp.float32)
     filter_tokens = filter_back.reshape(columns, rows).T
     passed = shifted(input_tokens[None], "pipe", -1)
     return (passed, filter_tokens[None])

time: 97.5 us -> 91 us (0.933)
  blocking collectives: 27.9 us -> 22.1 us
    all_to_all x1, blocking collectives: 27.9 us -> 22.1 us  [body(): lax.all_to_all(outgoing, 'seq', split_axis=1, concat_axis=1, tiled=True)]
where the time goes in v3:
time: 91 us; the launch traced here: 90.4 us
  waiting for transfers between devices  24.2 us (27%)
  blocking collectives  22.1 us (24%)
  matrix products  16.5 us (18%)
  starting transfers between devices  16 us (18%)
  local copies, waits for them, and re-layouts  9.72 us (11%)
  between operations  1.07 us (1%)
    all_to_all x1, waiting for transfers between devices, body(): recv = lax.all_to_all(send, 'seq', split_axis=1, concat_axis=1, tiled=True)  24.1 us
    all_to_all x1, blocking collectives, body(): lax.all_to_all(outgoing, 'seq', split_axis=1, concat_axis=1, tiled=True)  22.1 us
    all_to_all x1, starting transfers between devices, body(): recv = lax.all_to_all(send, 'seq', split_axis=1, concat_axis=1, tiled=True)  11.9 us
    unnamed x31, local copies, waits for them, and re-layouts  7.4 us
    dot_general x10, matrix products, contract(): jnp.einsum(form, jnp.asarray(table, jnp.float32), values, precision=PRECI...  4.57 us
    ppermute x1, starting transfers between devices, shifted(): return lax.ppermute(block, axis, route)  4.11 us
  transfers between devices with their start and end apart: 2, of which 2 were waited for; matrix products, arithmetic and copies ran while one was open for 2% of the time, Pallas kernels for 0%

profile of v3, /device:TPU:1, one launch (start us, length us, event | category | flops | bytes accessed | tf_op | source)
XLA Modules:
  0.0 90.4 jit_solution(13513276144692805239)
XLA Ops:
  0.6 1.1 %copy.97 = bf16[1,256,512]{1,2,0:T(8,128)(2,1)S(1)} copy(bf16[1,256,512]{2,1,0:T(8,128)(2,1)} %param.44) | data formatting | bytes 524288 | tf_op args[2]
  1.9 0.8 copy-done.5
  2.9 0.8 copy-done.6
  3.8 0.8 copy-done.7
  5.0 1.1 %copy.101 = bf16[4,32,16,256]{3,2,0,1:T(8,128)(2,1)} copy(bf16[4,32,16,256]{3,2,1,0:T(8,128)(2,1)S(1)} %bitcast.96) | data formatting | bytes 2097152 | tf_op jit(solution)/shard_map/reshape | solution.py:85
  6.2 11.9 %all-to-all-start = ((bf16[4,32,16,256]{3,2,0,1:T(8,128)(2,1)}), bf16[4,32,16,256]{3,2,0,1:T(8,128)(2,1)S(1)}, u32[]{:S(2)}, u32[]{:S(2)}) async-start(bf16[4,32,16,256]{3,2,0,1:T(8,128)(2,1)} %copy.101), calls=%async_computation | async-start | bytes 2097152 | tf_op jit(solution)/shard_map/all_to_all | solution.py:86
  18.0 0.8 fusion.67
  18.8 24.1 %all-to-all-done = bf16[4,32,16,256]{3,2,0,1:T(8,128)(2,1)S(1)} async-done(((bf16[4,32,16,256]{3,2,0,1:T(8,128)(2,1)}), bf16[4,32,16,256]{3,2,0,1:T(8,128)(2,1)S(1)}, u32[]{:S(2)}, u32[]{:S(2)}) %all-to-all-start) | async-done | bytes 1048608 | tf_op jit(solution)/shard_map/all_to_all | solution.py:86
  45.7 0.9 %multiply_add_fusion.1 = (f32[33,16,256]{2,0,1:T(8,128)S(1)}, f32[33,16,256]{2,0,1:T(8,128)S(1)}, f32[33,16,256]{2,0,1:T(8,128)S(1)}, f32[33,16,256]{2,0,1:T(8,1...) fusion(f32[33,16,256]{2,0,1:T(8,128)S(1)} %fusion.64, f32[33,256]{1,0:T(8,128)S(1)} %copy-done.2, ...), kind=kOutput, calls=%fused_computation.54 | convolution fusion | flops 28520448 | bytes 6281344 | tf_op jit(solution)/shard_map/ca,akr->ckr/dot_general | solution.py:25
  48.6 0.5 convolution_subtract_fusion.3
  52.2 0.5 convolution_add_fusion.2
  52.8 0.7 multiply_add_fusion.4
  53.5 0.7 fusion.17
  54.2 0.7 fusion.13
  54.9 0.7 convolution_subtract_fusion.1
  55.6 0.7 convolution_add_fusion.1
  57.6 0.8 fusion.7
  58.4 0.7 fusion.11
  59.1 0.7 convolution_add_fusion
  59.8 0.7 convolution_subtract_fusion
  62.1 22.1 %all_to_all.10 = bf16[2,32,16,256]{3,2,0,1:T(8,128)(2,1)S(1)} all-to-all(bf16[2,32,16,256]{3,2,0,1:T(8,128)(2,1)S(1)} %copy.126), channel_id=1, replica_groups=mesh['pipe'=2,'seq'=32,'chan'=4] {'seq'}, dimensions={1} | all-to-all | bytes 1048576 | tf_op jit(solution)/shard_map/all_to_all | solution.py:109
  84.3 4.1 %collective-permute-start = (bf16[1,256,512]{1,2,0:T(8,128)(2,1)S(1)}, bf16[1,256,512]{1,2,0:T(8,128)(2,1)S(1)}, u32[]{:S(2)}, u32[]{:S(2)}) collective-permute-start(bf16[1,256,512]{1,2,0:T(8,128)(2,1)S(1)} %bitcast.97), channel_id=1, source_target_pairs={{128,0},{0,128},{129,1},{1,129},{130,2},{2,130},{131,3},{3,131},{1... | collective-permute-start | bytes 786440 | tf_op jit(solution)/shard_map/ppermute | solution.py:16
  88.4 1.0 %copy.130 = f32[1,256,512]{2,1,0:T(8,128)} copy(f32[1,256,512]{1,2,0:T(8,128)S(1)} %convert_bitcast_fusion) | data formatting | bytes 1048576
  89.5 0.8 copy.129
  (54 shorter events, 11.6 us)
Async XLA Ops:
  0.6 1.1 %copy-start.4 = (bf16[1,256,512]{2,1,0:T(8,128)(2,1)S(1)}, bf16[1,256,512]{2,1,0:T(8,128)(2,1)}, u32[]{:S(2)}) copy-start(bf16[1,256,512]{2,1,0:T(8,128)(2,1)} %param.42) | copy-start | bytes 786436
  1.8 1.0 %copy-start.5 = (bf16[1,256,512]{2,1,0:T(8,128)(2,1)S(1)}, bf16[1,256,512]{2,1,0:T(8,128)(2,1)}, u32[]{:S(2)}) copy-start(bf16[1,256,512]{2,1,0:T(8,128)(2,1)} %param.43) | copy-start | bytes 786436
  2.7 0.9 %copy-start.6 = (bf16[1,256,512]{2,1,0:T(8,128)(2,1)S(1)}, bf16[1,256,512]{2,1,0:T(8,128)(2,1)}, u32[]{:S(2)}) copy-start(bf16[1,256,512]{2,1,0:T(8,128)(2,1)} %param.45) | copy-start | bytes 786436
  3.7 0.9 %copy-start.7 = (bf16[1,256,512]{2,1,0:T(8,128)(2,1)S(1)}, bf16[1,256,512]{2,1,0:T(8,128)(2,1)}, u32[]{:S(2)}) copy-start(bf16[1,256,512]{2,1,0:T(8,128)(2,1)} %param.47) | copy-start | bytes 786436
  6.2 36.7 %all-to-all-start = ((bf16[4,32,16,256]{3,2,0,1:T(8,128)(2,1)}), bf16[4,32,16,256]{3,2,0,1:T(8,128)(2,1)S(1)}, u32[]{:S(2)}, u32[]{:S(2)}) async-start(bf16[4,32,16,256]{3,2,0,1:T(8,128)(2,1)} %copy.101), calls=%async_computation | async-start | bytes 2097152 | tf_op jit(solution)/shard_map/all_to_all | solution.py:86
  18.8 24.2 %copy-start.9 = (f32[33,32,1]{0,1,2:T(8,128)S(1)}, f32[33,32,1]{0,1,2:T(8,128)}, u32[]{:S(2)}) copy-start(f32[33,32,1]{0,1,2:T(8,128)} %constant.48) | copy-start | bytes 12676
  43.0 0.7 copy-start.8
  44.9 0.8 copy-start.2
  44.9 0.8 copy-start.3
  45.7 0.9 %copy-start.1 = (f32[256,256,1]{1,0,2:T(8,128)S(1)}, f32[256,256,1]{1,0,2:T(8,128)}, u32[]{:S(2)}) copy-start(f32[256,256,1]{1,0,2:T(8,128)} %constant.49) | copy-start | bytes 786436
  47.2 1.0 %copy-start = (f32[256,256,1]{1,0,2:T(8,128)S(1)}, f32[256,256,1]{1,0,2:T(8,128)}, u32[]{:S(2)}) copy-start(f32[256,256,1]{1,0,2:T(8,128)} %constant.50) | copy-start | bytes 786436
  55.6 0.7 copy-start.11
  56.3 0.7 copy-start.10
  84.3 5.3 %collective-permute-start = (bf16[1,256,512]{1,2,0:T(8,128)(2,1)S(1)}, bf16[1,256,512]{1,2,0:T(8,128)(2,1)S(1)}, u32[]{:S(2)}, u32[]{:S(2)}) collective-permute-start(bf16[1,256,512]{1,2,0:T(8,128)(2,1)S(1)} %bitcast.97), channel_id=1, source_target_pairs={{128,0},{0,128},{129,1},{1,129},{130,2},{2,130},{131,3},{3,131},{1... | collective-permute-start | bytes 786440 | tf_op jit(solution)/shard_map/ppermute | solution.py:16

commit v4 on v3

--- a/solution.py
+++ b/solution.py
@@ -25,52 +25,42 @@
     return jnp.einsum(form, jnp.asarray(table, jnp.float32), values, precision=PRECISION)
 
 
-def forward(signal, padded):
-    blocks, _, rows = signal.shape
+def forward(signals, padded):
+    _, blocks, _, rows = signals.shape
     half = np.arange(blocks + 1)
     cos_b, sin_b = angle_table(half, np.arange(blocks), 2 * blocks)
-    real = contract("ca,akr->ckr", cos_b, signal)
-    imag = -contract("ca,akr->ckr", sin_b, signal)
+    first = contract("ja,sakr->sjkr", np.concatenate([cos_b, -sin_b]), signals)
+    real, imag = first[:, : blocks + 1], first[:, blocks + 1 :]
     cos_t, sin_t = angle_table(half, np.arange(rows), padded)
     cos_t = jnp.asarray(cos_t, jnp.float32)[:, None, :]
     sin_t = jnp.asarray(sin_t, jnp.float32)[:, None, :]
-    twisted_real = real * cos_t + imag * sin_t
-    twisted_imag = imag * cos_t - real * sin_t
+    twisted = jnp.concatenate([real * cos_t + imag * sin_t, imag * cos_t - real * sin_t], axis=-1)
     cos_r, sin_r = angle_table(np.arange(rows), np.arange(rows), rows)
-    out_real = jnp.einsum("ckr,rd->ckd", twisted_real, jnp.asarray(cos_r, jnp.float32), precision=PRECISION) + jnp.einsum(
-        "ckr,rd->ckd", twisted_imag, jnp.asarray(sin_r, jnp.float32), precision=PRECISION
-    )
-    out_imag = jnp.einsum("ckr,rd->ckd", twisted_imag, jnp.asarray(cos_r, jnp.float32), precision=PRECISION) - jnp.einsum(
-        "ckr,rd->ckd", twisted_real, jnp.asarray(sin_r, jnp.float32), precision=PRECISION
-    )
-    return out_real, out_imag
+    table = np.block([[cos_r, -sin_r], [sin_r, cos_r]])
+    spectrum = contract("rd,shkr->shkd", table, twisted)
+    return spectrum[..., :rows], spectrum[..., rows:]
 
 
 def inverse(real, imag, padded):
-    half_count, _, rows = real.shape
+    _, half_count, _, rows = real.shape
     blocks = half_count - 1
     half = np.arange(half_count)
     cos_r, sin_r = angle_table(np.arange(rows), np.arange(rows), rows)
-    cos_r = jnp.asarray(cos_r, jnp.float32)
-    sin_r = jnp.asarray(sin_r, jnp.float32)
-    back_real = jnp.einsum("ckd,dr->ckr", real, cos_r, precision=PRECISION) - jnp.einsum(
-        "ckd,dr->ckr", imag, sin_r, precision=PRECISION
-    )
-    back_imag = jnp.einsum("ckd,dr->ckr", imag, cos_r, precision=PRECISION) + jnp.einsum(
-        "ckd,dr->ckr", real, sin_r, precision=PRECISION
-    )
+    table = np.block([[cos_r, sin_r], [-sin_r, cos_r]])
+    back = contract("dr,shkd->shkr", table, jnp.concatenate([real, imag], axis=-1))
+    back_real, back_imag = back[..., :rows], back[..., rows:]
     cos_t, sin_t = angle_table(half, np.arange(rows), padded)
     cos_t = jnp.asarray(cos_t, jnp.float32)[:, None, :]
     sin_t = jnp.asarray(sin_t, jnp.float32)[:, None, :]
-    twisted_real = back_real * cos_t - back_imag * sin_t
-    twisted_imag = back_imag * cos_t + back_real * sin_t
+    twisted = jnp.concatenate(
+        [back_real * cos_t - back_imag * sin_t, back_imag * cos_t + back_real * sin_t], axis=1
+    )
     weight = np.full(half_count, 2.0)
     weight[0] = 1.0
     weight[blocks] = 1.0
     cos_b, sin_b = angle_table(np.arange(blocks), half, 2 * blocks)
-    cos_b = cos_b * weight[None, :] / padded
-    sin_b = sin_b * weight[None, :] / padded
-    return contract("ac,ckr->akr", cos_b, twisted_real) - contract("ac,ckr->akr", sin_b, twisted_imag)
+    table_b = np.concatenate([cos_b, -sin_b], axis=1) * np.concatenate([weight, weight])[None, :] / padded
+    return contract("ac,sckr->sakr", table_b, twisted)
 
 
 def body(grad_out, value_branch, key_gate, query_gate, short_weights, long_filters):
@@ -84,15 +74,16 @@
     stacked = jnp.stack([grad_conv, gated_value, long_filters[0], key_gate[0]])
     send = jnp.swapaxes(stacked, 1, 2).reshape(4, devices, group, rows)
     recv = lax.all_to_all(send, "seq", split_axis=1, concat_axis=1, tiled=True)
-    conv_real, conv_imag = forward(recv[0].astype(jnp.float32), padded)
-    gated_real, gated_imag = forward(recv[1].astype(jnp.float32), padded)
-    filter_real, filter_imag = forward(recv[2].astype(jnp.float32), padded)
+    spec_real, spec_imag = forward(recv[:3].astype(jnp.float32), padded)
+    conv_real, conv_imag = spec_real[0], spec_imag[0]
+    gated_real, gated_imag = spec_real[1], spec_imag[1]
+    filter_real, filter_imag = spec_real[2], spec_imag[2]
     back_real = conv_real * filter_real + conv_imag * filter_imag
     back_imag = conv_imag * filter_real - conv_real * filter_imag
     fold_real = conv_real * gated_real + conv_imag * gated_imag
     fold_imag = conv_imag * gated_real - conv_real * gated_imag
-    grad_gated = inverse(back_real, back_imag, padded)
-    grad_filter = inverse(fold_real, fold_imag, padded)
+    both = inverse(jnp.stack([back_real, fold_real]), jnp.stack([back_imag, fold_imag]), padded)
+    grad_gated, grad_filter = both[0], both[1]
     grad_value = recv[3].astype(jnp.float32) * grad_gated
     rim = jnp.concatenate(
         [grad_value[1:, :, :2], jnp.zeros((1, group, 2), grad_value.dtype)], axis=0

time: 91 us -> 86.6 us (0.952)
  matrix products: 16.5 us -> 9.06 us
  other arithmetic: 0.83 us -> 3 us
  local copies, waits for them, and re-layouts: 9.72 us -> 10.7 us
    dot_general x20 -> x0, matrix products: 11.9 us -> none  [the longest x3 1.75 us: forward(): jnp.einsum('ckr,rd->ckd', twisted_real, jnp.asarray(sin_r, jnp.float32),...]
    dot_general x10 -> x4, matrix products: 4.57 us -> 9.06 us  [contract(): jnp.einsum(form, jnp.asarray(table, jnp.float32), values, precision=PRECI...]
    unnamed x31 -> x21, local copies, waits for them, and re-layouts: 7.4 us -> 8.35 us
where the time goes in v4:
time: 86.6 us; the launch traced here: 86.1 us
  waiting for transfers between devices  24.2 us (28%)
  blocking collectives  22.1 us (26%)
  starting transfers between devices  16.1 us (19%)
  local copies, waits for them, and re-layouts  10.7 us (12%)
  matrix products  9.06 us (10%)
  other arithmetic  3 us (3%)
  between operations  0.92 us (1%)
    all_to_all x1, waiting for transfers between devices, body(): recv = lax.all_to_all(send, 'seq', split_axis=1, concat_axis=1, tiled=True)  24.1 us
    all_to_all x1, blocking collectives, body(): lax.all_to_all(outgoing, 'seq', split_axis=1, concat_axis=1, tiled=True)  22.1 us
    all_to_all x1, starting transfers between devices, body(): recv = lax.all_to_all(send, 'seq', split_axis=1, concat_axis=1, tiled=True)  12 us
    dot_general x4, matrix products, contract(): jnp.einsum(form, jnp.asarray(table, jnp.float32), values, precision=PRECI...  9.06 us
    unnamed x21, local copies, waits for them, and re-layouts  8.35 us
    ppermute x1, starting transfers between devices, shifted(): return lax.ppermute(block, axis, route)  4.11 us
  transfers between devices with their start and end apart: 2, of which 2 were waited for; matrix products, arithmetic and copies ran while one was open for 2% of the time, Pallas kernels for 0%

profile of v4, /device:TPU:1, one launch (start us, length us, event | category | flops | bytes accessed | tf_op | source)
XLA Modules:
  0.0 86.1 jit_solution(16242548050449713779)
XLA Ops:
  0.6 1.1 %copy.33 = bf16[1,256,512]{1,2,0:T(8,128)(2,1)S(1)} copy(bf16[1,256,512]{2,1,0:T(8,128)(2,1)} %param.16) | data formatting | bytes 524288 | tf_op args[2]
  1.8 1.1 %copy.32 = bf16[1,256,512]{1,2,0:T(8,128)(2,1)S(1)} copy(bf16[1,256,512]{2,1,0:T(8,128)(2,1)} %param.14) | data formatting | bytes 524288 | tf_op args[0]
  2.9 1.1 %copy.34 = bf16[1,256,512]{1,2,0:T(8,128)(2,1)S(1)} copy(bf16[1,256,512]{2,1,0:T(8,128)(2,1)} %param.15) | data formatting | bytes 524288 | tf_op args[1]
  4.0 1.1 %copy.31 = bf16[1,256,512]{1,2,0:T(8,128)(2,1)S(1)} copy(bf16[1,256,512]{2,1,0:T(8,128)(2,1)} %param.17) | data formatting | bytes 524288 | tf_op args[3]
  5.5 1.1 %copy.37 = bf16[4,32,16,256]{3,2,0,1:T(8,128)(2,1)} copy(bf16[4,32,16,256]{3,2,1,0:T(8,128)(2,1)S(1)} %bitcast.49) | data formatting | bytes 2097152 | tf_op jit(solution)/shard_map/reshape | solution.py:75
  6.6 12.0 %all-to-all-start = ((bf16[4,32,16,256]{3,2,0,1:T(8,128)(2,1)}), bf16[4,32,16,256]{3,2,0,1:T(8,128)(2,1)S(1)}, u32[]{:S(2)}, u32[]{:S(2)}) async-start(bf16[4,32,16,256]{3,2,0,1:T(8,128)(2,1)} %copy.37), calls=%async_computation | async-start | bytes 2097152 | tf_op jit(solution)/shard_map/all_to_all | solution.py:76
  18.6 0.8 fusion.22
  19.4 24.1 %all-to-all-done = bf16[4,32,16,256]{3,2,0,1:T(8,128)(2,1)S(1)} async-done(((bf16[4,32,16,256]{3,2,0,1:T(8,128)(2,1)}), bf16[4,32,16,256]{3,2,0,1:T(8,128)(2,1)S(1)}, u32[]{:S(2)}, u32[]{:S(2)}) %all-to-all-start) | async-done | bytes 1048608 | tf_op jit(solution)/shard_map/all_to_all | solution.py:76
  43.6 1.1 %convolution_bitcast_fusion = f32[3,66,16,256]{3,1,2,0:T(8,128)S(1)} fusion(f32[66,32,1,1]{0,1,3,2:T(8,128)S(1)} %copy-done.6, bf16[3,32,16,256]{3,2,0,1:T(8,128)(2,1)S(1)} %slice.101), kind=kOutput, calls=%fused_computation.14 | convolution fusion | flops 155713536 | bytes 4038912 | tf_op jit(solution)/shard_map/ja,sakr->sjkr/dot_general | solution.py:25
  44.7 0.5 multiply_add_fusion
  45.3 0.6 pad_maximum_fusion
  45.9 0.6 copy-done
  46.5 4.1 %fusion = f32[3,33,16,512]{3,2,1,0:T(8,128)S(1)} fusion(f32[512,512,1,1]{1,0,3,2:T(8,128)S(1)} %copy-done, f32[3,33,16,512]{3,1,2,0:T(8,128)S(1)} %pad_maximum_fusion), kind=kOutput, calls=%fused_computation.1 | convolution fusion | flops 2491416576 | bytes 7536640 | tf_op jit(solution)/shard_map/rd,shkr->shkd/dot_general | solution.py:25
  50.6 0.4 multiply_add_fusion.3
  51.0 0.8 copy-done.1
  51.8 1.9 %fusion.4 = f32[2,33,16,512]{3,2,1,0:T(8,128)S(1)} fusion(f32[512,512,1,1]{1,0,3,2:T(8,128)S(1)} %copy-done.1, f32[1,33,16,256]{3,2,1,0:T(8,128)S(1)} %get-tuple-element.11, f32[1,33,16,256]{3,2,1,0:T(8,128)S(1)} %get-tuple-element.10, f32[1,33,16,256]{3,2,1,0:T(8,128)S(1)} %get-tuple-element.9, f32[1,33,16,256]{3,2,1,0:T(8,128)S(1)} %get-tuple-element.8), kind=kOutput, calls=%fused_computation.5 | convolution fusion | flops 1662566400 | bytes 5373952 | tf_op jit(solution)/shard_map/dr,shkd->shkr/dot_general | solution.py:25
  53.7 0.3 multiply_subtract_fusion.1
  54.3 0.5 copy-done.5
  54.8 1.9 %fusion.12 = f32[2,32,16,256]{3,1,2,0:T(8,128)S(1)} fusion(f32[32,66,1,1]{1,0,3,2:T(8,128)S(1)} %copy-done.5, f32[2,66,16,256]{3,2,1,0:T(8,128)S(1)} %pad_maximum_fusion.1), kind=kOutput, calls=%fused_computation.17 | convolution fusion | flops 103809024 | bytes 3219712 | tf_op jit(solution)/shard_map/ac,sckr->sakr/dot_general | solution.py:25
  57.1 0.4 fusion.20
  57.8 22.1 %all_to_all.10 = bf16[2,32,16,256]{3,2,0,1:T(8,128)(2,1)S(1)} all-to-all(bf16[2,32,16,256]{3,2,0,1:T(8,128)(2,1)S(1)} %copy.42), channel_id=1, replica_groups=mesh['pipe'=2,'seq'=32,'chan'=4] {'seq'}, dimensions={1} | all-to-all | bytes 1048576 | tf_op jit(solution)/shard_map/all_to_all | solution.py:100
  80.0 4.1 %collective-permute-start = (bf16[1,256,512]{1,2,0:T(8,128)(2,1)S(1)}, bf16[1,256,512]{1,2,0:T(8,128)(2,1)S(1)}, u32[]{:S(2)}, u32[]{:S(2)}) collective-permute-start(bf16[1,256,512]{1,2,0:T(8,128)(2,1)S(1)} %bitcast.50), channel_id=1, source_target_pairs={{128,0},{0,128},{129,1},{1,129},{130,2},{2,130},{131,3},{3,131},{1... | collective-permute-start | bytes 786440 | tf_op jit(solution)/shard_map/ppermute | solution.py:16
  84.1 1.0 %copy.46 = f32[1,256,512]{2,1,0:T(8,128)} copy(f32[1,256,512]{1,2,0:T(8,128)S(1)} %convert_bitcast_fusion) | data formatting | bytes 1048576
  85.3 0.8 copy.45
  (26 shorter events, 1.5 us)
Async XLA Ops:
  0.6 4.4 %copy-start.2 = (bf16[1,256,512]{2,1,0:T(8,128)(2,1)S(1)}, bf16[1,256,512]{2,1,0:T(8,128)(2,1)}, u32[]{:S(2)}) copy-start(bf16[1,256,512]{2,1,0:T(8,128)(2,1)} %param.19) | copy-start | bytes 786436
  6.6 36.9 %copy-start.6 = (f32[66,32,1,1]{0,1,3,2:T(8,128)S(1)}, f32[66,32,1,1]{0,1,3,2:T(8,128)}, u32[]{:S(2)}) copy-start(f32[66,32,1,1]{0,1,3,2:T(8,128)} %constant.41) | copy-start | bytes 25348
  6.6 36.9 %all-to-all-start = ((bf16[4,32,16,256]{3,2,0,1:T(8,128)(2,1)}), bf16[4,32,16,256]{3,2,0,1:T(8,128)(2,1)S(1)}, u32[]{:S(2)}, u32[]{:S(2)}) async-start(bf16[4,32,16,256]{3,2,0,1:T(8,128)(2,1)} %copy.37), calls=%async_computation | async-start | bytes 2097152 | tf_op jit(solution)/shard_map/all_to_all | solution.py:76
  43.5 1.2 %copy-start.3 = (f32[33,256]{1,0:T(8,128)S(1)}, f32[33,256]{1,0:T(8,128)}, u32[]{:S(2)}) copy-start(f32[33,256]{1,0:T(8,128)} %constant.29.clone) | copy-start | bytes 101380
  43.5 1.2 %copy-start.4 = (f32[33,256]{1,0:T(8,128)S(1)}, f32[33,256]{1,0:T(8,128)}, u32[]{:S(2)}) copy-start(f32[33,256]{1,0:T(8,128)} %constant.28.clone) | copy-start | bytes 101380
  45.3 1.2 %copy-start = (f32[512,512,1,1]{1,0,3,2:T(8,128)S(1)}, f32[512,512,1,1]{1,0,3,2:T(8,128)}, u32[]{:S(2)}) copy-start(f32[512,512,1,1]{1,0,3,2:T(8,128)} %constant.42) | copy-start | bytes 3145732
  50.6 1.2 %copy-start.1 = (f32[512,512,1,1]{1,0,3,2:T(8,128)S(1)}, f32[512,512,1,1]{1,0,3,2:T(8,128)}, u32[]{:S(2)}) copy-start(f32[512,512,1,1]{1,0,3,2:T(8,128)} %constant.43) | copy-start | bytes 3145732
  54.1 0.7 copy-start.5
  80.0 5.3 %collective-permute-start = (bf16[1,256,512]{1,2,0:T(8,128)(2,1)S(1)}, bf16[1,256,512]{1,2,0:T(8,128)(2,1)S(1)}, u32[]{:S(2)}, u32[]{:S(2)}) collective-permute-start(bf16[1,256,512]{1,2,0:T(8,128)(2,1)S(1)} %bitcast.50), channel_id=1, source_target_pairs={{128,0},{0,128},{129,1},{1,129},{130,2},{2,130},{131,3},{3,131},{1... | collective-permute-start | bytes 786440 | tf_op jit(solution)/shard_map/ppermute | solution.py:16

commit v5 on v4

--- a/solution.py
+++ b/solution.py
@@ -71,9 +71,11 @@
     padded = 2 * rows * devices
     grad_conv = (query_gate[0].astype(jnp.float32) * grad_out[0].astype(jnp.float32)).astype(jnp.bfloat16)
     gated_value = (key_gate[0].astype(jnp.float32) * value_branch[0].astype(jnp.float32)).astype(jnp.bfloat16)
-    stacked = jnp.stack([grad_conv, gated_value, long_filters[0], key_gate[0]])
-    send = jnp.swapaxes(stacked, 1, 2).reshape(4, devices, group, rows)
+    stacked = jnp.stack([grad_conv, gated_value, long_filters[0]])
+    send = jnp.swapaxes(stacked, 1, 2).reshape(3, devices, group, rows)
     recv = lax.all_to_all(send, "seq", split_axis=1, concat_axis=1, tiled=True)
+    key_send = key_gate[0].T.reshape(devices, group, rows)
+    key_recv = lax.all_to_all(key_send, "seq", split_axis=0, concat_axis=0, tiled=True)
     spec_real, spec_imag = forward(recv[:3].astype(jnp.float32), padded)
     conv_real, conv_imag = spec_real[0], spec_imag[0]
     gated_real, gated_imag = spec_real[1], spec_imag[1]
@@ -84,7 +86,7 @@
     fold_imag = conv_imag * gated_real - conv_real * gated_imag
     both = inverse(jnp.stack([back_real, fold_real]), jnp.stack([back_imag, fold_imag]), padded)
     grad_gated, grad_filter = both[0], both[1]
-    grad_value = recv[3].astype(jnp.float32) * grad_gated
+    grad_value = key_recv.astype(jnp.float32) * grad_gated
     rim = jnp.concatenate(
         [grad_value[1:, :, :2], jnp.zeros((1, group, 2), grad_value.dtype)], axis=0
     )

time: 86.6 us -> 91.7 us (1.059)
  starting transfers between devices: 16.1 us -> 25.3 us
  waiting for transfers between devices: 24.2 us -> 18.7 us
    all_to_all x0 -> x1, starting transfers between devices: none -> 8.25 us  [body(): lax.all_to_all(key_send, 'seq', split_axis=0, concat_axis=0, tiled=True)]
    all_to_all x1, waiting for transfers between devices: 24.1 us -> 18.6 us  [body(): recv = lax.all_to_all(send, 'seq', split_axis=1, concat_axis=1, tiled=True)]
    ppermute x1, starting transfers between devices: 4.11 us -> 5.15 us  [shifted(): return lax.ppermute(block, axis, route)]
  transfers between devices with their start and end apart: 2 -> 3, of which waited for: 2 -> 2; matrix products, arithmetic and copies ran while one was open for 2% -> 14% of each run, Pallas kernels for 0% -> 0%
where the time goes in v5:
time: 91.7 us; the launch traced here: 91.1 us
  starting transfers between devices  25.3 us (28%)
  blocking collectives  22.1 us (24%)
  waiting for transfers between devices  18.7 us (20%)
  local copies, waits for them, and re-layouts  11.2 us (12%)
  matrix products  9.07 us (10%)
  other arithmetic  3.89 us (4%)
  between operations  0.93 us (1%)
    all_to_all x1, blocking collectives, body(): lax.all_to_all(outgoing, 'seq', split_axis=1, concat_axis=1, tiled=True)  22.1 us
    all_to_all x1, waiting for transfers between devices, body(): recv = lax.all_to_all(send, 'seq', split_axis=1, concat_axis=1, tiled=True)  18.6 us
    all_to_all x1, starting transfers between devices, body(): recv = lax.all_to_all(send, 'seq', split_axis=1, concat_axis=1, tiled=True)  11.9 us
    dot_general x4, matrix products, contract(): jnp.einsum(form, jnp.asarray(table, jnp.float32), values, precision=PRECI...  9.07 us
    unnamed x21, local copies, waits for them, and re-layouts  9.06 us
    all_to_all x1, starting transfers between devices, body(): lax.all_to_all(key_send, 'seq', split_axis=0, concat_axis=0, tiled=True)  8.25 us
    ppermute x1, starting transfers between devices, shifted(): return lax.ppermute(block, axis, route)  5.15 us
  transfers between devices with their start and end apart: 3, of which 2 were waited for; matrix products, arithmetic and copies ran while one was open for 14% of the time, Pallas kernels for 0%

profile of v5, /device:TPU:1, one launch (start us, length us, event | category | flops | bytes accessed | tf_op | source)
XLA Modules:
  0.0 91.1 jit_solution(1813647975172038530)
XLA Ops:
  0.6 1.8 %copy.32 = bf16[1,256,512]{1,2,0:T(8,128)(2,1)} copy(bf16[1,256,512]{2,1,0:T(8,128)(2,1)} %param.16) | data formatting | bytes 524288 | tf_op args[2]
  2.5 1.1 %copy.37 = bf16[1,256,512]{1,2,0:T(8,128)(2,1)S(1)} copy(bf16[1,256,512]{2,1,0:T(8,128)(2,1)} %param.15) | data formatting | bytes 524288 | tf_op args[1]
  3.6 1.1 %copy.34 = bf16[1,256,512]{1,2,0:T(8,128)(2,1)S(1)} copy(bf16[1,256,512]{2,1,0:T(8,128)(2,1)} %param.17) | data formatting | bytes 524288 | tf_op args[3]
  4.7 1.1 %copy.35 = bf16[1,256,512]{1,2,0:T(8,128)(2,1)S(1)} copy(bf16[1,256,512]{2,1,0:T(8,128)(2,1)} %param.14) | data formatting | bytes 524288 | tf_op args[0]
  5.9 1.0 %multiply_convert_fusion = bf16[1,256,512]{1,2,0:T(8,128)(2,1)S(1)} fusion(bf16[1,256,512]{1,2,0:T(8,128)(2,1)S(1)} %copy.37, bf16[1,256,512]{1,2,0:T(8,128)(2,1)} %copy.32), kind=kLoop, calls=%fused_computation.38 | loop fusion | flops 524288 | bytes 786432 | tf_op jit(solution)/shard_map/convert_element_type | solution.py:73
  7.1 1.0 %copy.39 = bf16[3,32,16,256]{3,2,0,1:T(8,128)(2,1)} copy(bf16[3,32,16,256]{3,2,1,0:T(8,128)(2,1)S(1)} %bitcast.56) | data formatting | bytes 1572864 | tf_op jit(solution)/shard_map/reshape | solution.py:75
  8.0 11.9 %all-to-all-start.1 = ((bf16[3,32,16,256]{3,2,0,1:T(8,128)(2,1)}), bf16[3,32,16,256]{3,2,0,1:T(8,128)(2,1)S(1)}, u32[]{:S(2)}, u32[]{:S(2)}) async-start(bf16[3,32,16,256]{3,2,0,1:T(8,128)(2,1)} %copy.39), calls=%async_computation.1 | async-start | bytes 1572864 | tf_op jit(solution)/shard_map/all_to_all | solution.py:76
  19.9 0.8 fusion.22
  20.7 18.6 %all-to-all-done.1 = bf16[3,32,16,256]{3,2,0,1:T(8,128)(2,1)S(1)} async-done(((bf16[3,32,16,256]{3,2,0,1:T(8,128)(2,1)}), bf16[3,32,16,256]{3,2,0,1:T(8,128)(2,1)S(1)}, u32[]{:S(2)}, u32[]{:S(2)}) %all-to-all-start.1) | async-done | bytes 786464 | tf_op jit(solution)/shard_map/all_to_all | solution.py:76
  39.3 8.2 %all-to-all-start = ((bf16[32,16,256]{2,1,0:T(8,128)(2,1)}), bf16[32,16,256]{2,1,0:T(8,128)(2,1)S(1)}, u32[]{:S(2)}, u32[]{:S(2)}) async-start(bf16[32,16,256]{2,1,0:T(8,128)(2,1)} %bitcast.3), calls=%async_computation | async-start | bytes 524288 | tf_op jit(solution)/shard_map/all_to_all | solution.py:78
  47.6 1.1 %convolution_bitcast_fusion = f32[3,66,16,256]{3,1,2,0:T(8,128)S(1)} fusion(f32[66,32,1,1]{0,1,3,2:T(8,128)S(1)} %copy-done.6, bf16[3,32,16,256]{3,2,0,1:T(8,128)(2,1)S(1)} %all-to-all-done.1), kind=kOutput, calls=%fused_computation.14 | convolution fusion | flops 155713536 | bytes 4038912 | tf_op jit(solution)/shard_map/ja,sakr->sjkr/dot_general | solution.py:25
  48.7 0.5 multiply_add_fusion
  49.3 0.6 pad_maximum_fusion
  49.9 0.6 copy-done
  50.5 4.1 %fusion = f32[3,33,16,512]{3,2,1,0:T(8,128)S(1)} fusion(f32[512,512,1,1]{1,0,3,2:T(8,128)S(1)} %copy-done, f32[3,33,16,512]{3,1,2,0:T(8,128)S(1)} %pad_maximum_fusion), kind=kOutput, calls=%fused_computation.1 | convolution fusion | flops 2491416576 | bytes 7536640 | tf_op jit(solution)/shard_map/rd,shkr->shkd/dot_general | solution.py:25
  55.0 0.8 copy-done.1
  55.9 1.9 %fusion.4 = f32[2,33,16,512]{3,2,1,0:T(8,128)S(1)} fusion(f32[512,512,1,1]{1,0,3,2:T(8,128)S(1)} %copy-done.1, f32[1,33,16,256]{3,2,1,0:T(8,128)S(1)} %get-tuple-element.11, f32[1,33,16,256]{3,2,1,0:T(8,128)S(1)} %get-tuple-element.10, f32[1,33,16,256]{3,2,1,0:T(8,128)S(1)} %get-tuple-element.9, f32[1,33,16,256]{3,2,1,0:T(8,128)S(1)} %get-tuple-element.8), kind=kOutput, calls=%fused_computation.5 | convolution fusion | flops 1662566400 | bytes 5373952 | tf_op jit(solution)/shard_map/dr,shkd->shkr/dot_general | solution.py:25
  58.3 0.5 copy-done.5
  58.9 1.9 %fusion.12 = f32[2,32,16,256]{3,1,2,0:T(8,128)S(1)} fusion(f32[32,66,1,1]{1,0,3,2:T(8,128)S(1)} %copy-done.5, f32[2,66,16,256]{3,2,1,0:T(8,128)S(1)} %pad_maximum_fusion.1), kind=kOutput, calls=%fused_computation.17 | convolution fusion | flops 103809024 | bytes 3219712 | tf_op jit(solution)/shard_map/ac,sckr->sakr/dot_general | solution.py:25
  61.0 0.4 fusion.20
  61.8 22.1 %all_to_all.15 = bf16[2,32,16,256]{3,2,0,1:T(8,128)(2,1)S(1)} all-to-all(bf16[2,32,16,256]{3,2,0,1:T(8,128)(2,1)S(1)} %copy.43), channel_id=1, replica_groups=mesh['pipe'=2,'seq'=32,'chan'=4] {'seq'}, dimensions={1} | all-to-all | bytes 1048576 | tf_op jit(solution)/shard_map/all_to_all | solution.py:102
  84.0 5.2 %collective-permute-start = (bf16[1,256,512]{1,2,0:T(8,128)(2,1)S(1)}, bf16[1,256,512]{1,2,0:T(8,128)(2,1)S(1)}, u32[]{:S(2)}, u32[]{:S(2)}) collective-permute-start(bf16[1,256,512]{1,2,0:T(8,128)(2,1)S(1)} %bitcast.57), channel_id=1, source_target_pairs={{128,0},{0,128},{129,1},{1,129},{130,2},{2,130},{131,3},{3,131},{1... | collective-permute-start | bytes 786440 | tf_op jit(solution)/shard_map/ppermute | solution.py:16
  89.2 1.0 %copy.47 = f32[1,256,512]{2,1,0:T(8,128)} copy(f32[1,256,512]{1,2,0:T(8,128)S(1)} %convert_bitcast_fusion) | data formatting | bytes 1048576
  90.3 0.8 copy.46
  (27 shorter events, 2.0 us)
Async XLA Ops:
  0.6 5.1 %copy-start.2 = (bf16[1,256,512]{2,1,0:T(8,128)(2,1)S(1)}, bf16[1,256,512]{2,1,0:T(8,128)(2,1)}, u32[]{:S(2)}) copy-start(bf16[1,256,512]{2,1,0:T(8,128)(2,1)} %param.19) | copy-start | bytes 786436
  7.1 40.5 %copy-start.6 = (f32[66,32,1,1]{0,1,3,2:T(8,128)S(1)}, f32[66,32,1,1]{0,1,3,2:T(8,128)}, u32[]{:S(2)}) copy-start(f32[66,32,1,1]{0,1,3,2:T(8,128)} %constant.41) | copy-start | bytes 25348
  8.0 31.2 %all-to-all-start.1 = ((bf16[3,32,16,256]{3,2,0,1:T(8,128)(2,1)}), bf16[3,32,16,256]{3,2,0,1:T(8,128)(2,1)S(1)}, u32[]{:S(2)}, u32[]{:S(2)}) async-start(bf16[3,32,16,256]{3,2,0,1:T(8,128)(2,1)} %copy.39), calls=%async_computation.1 | async-start | bytes 1572864 | tf_op jit(solution)/shard_map/all_to_all | solution.py:76
  39.3 21.6 %all-to-all-start = ((bf16[32,16,256]{2,1,0:T(8,128)(2,1)}), bf16[32,16,256]{2,1,0:T(8,128)(2,1)S(1)}, u32[]{:S(2)}, u32[]{:S(2)}) async-start(bf16[32,16,256]{2,1,0:T(8,128)(2,1)} %bitcast.3), calls=%async_computation | async-start | bytes 524288 | tf_op jit(solution)/shard_map/all_to_all | solution.py:78
  47.5 1.2 %copy-start.3 = (f32[33,256]{1,0:T(8,128)S(1)}, f32[33,256]{1,0:T(8,128)}, u32[]{:S(2)}) copy-start(f32[33,256]{1,0:T(8,128)} %constant.28.clone) | copy-start | bytes 101380
  47.5 1.2 %copy-start.4 = (f32[33,256]{1,0:T(8,128)S(1)}, f32[33,256]{1,0:T(8,128)}, u32[]{:S(2)}) copy-start(f32[33,256]{1,0:T(8,128)} %constant.29.clone) | copy-start | bytes 101380
  49.3 1.2 %copy-start = (f32[512,512,1,1]{1,0,3,2:T(8,128)S(1)}, f32[512,512,1,1]{1,0,3,2:T(8,128)}, u32[]{:S(2)}) copy-start(f32[512,512,1,1]{1,0,3,2:T(8,128)} %constant.42) | copy-start | bytes 3145732
  54.6 1.2 %copy-start.1 = (f32[512,512,1,1]{1,0,3,2:T(8,128)S(1)}, f32[512,512,1,1]{1,0,3,2:T(8,128)}, u32[]{:S(2)}) copy-start(f32[512,512,1,1]{1,0,3,2:T(8,128)} %constant.43) | copy-start | bytes 3145732
  58.1 0.7 copy-start.5
  84.0 6.3 %collective-permute-start = (bf16[1,256,512]{1,2,0:T(8,128)(2,1)S(1)}, bf16[1,256,512]{1,2,0:T(8,128)(2,1)S(1)}, u32[]{:S(2)}, u32[]{:S(2)}) collective-permute-start(bf16[1,256,512]{1,2,0:T(8,128)(2,1)S(1)} %bitcast.57), channel_id=1, source_target_pairs={{128,0},{0,128},{129,1},{1,129},{130,2},{2,130},{131,3},{3,131},{1... | collective-permute-start | bytes 786440 | tf_op jit(solution)/shard_map/ppermute | solution.py:16

commit v6 on v4

--- a/solution.py
+++ b/solution.py
@@ -25,7 +25,16 @@
     return jnp.einsum(form, jnp.asarray(table, jnp.float32), values, precision=PRECISION)
 
 
-def forward(signals, padded):
+def row_table(rows):
+    index = lax.optimization_barrier(jnp.arange(rows, dtype=jnp.int32))
+    angles = ((index[:, None] * index[None, :]) % rows).astype(jnp.float32) * (2.0 * math.pi / rows)
+    cos_r, sin_r = jnp.cos(angles), jnp.sin(angles)
+    return jnp.concatenate(
+        [jnp.concatenate([cos_r, -sin_r], axis=1), jnp.concatenate([sin_r, cos_r], axis=1)], axis=0
+    )
+
+
+def forward(signals, table, padded):
     _, blocks, _, rows = signals.shape
     half = np.arange(blocks + 1)
     cos_b, sin_b = angle_table(half, np.arange(blocks), 2 * blocks)
@@ -35,19 +44,17 @@
     cos_t = jnp.asarray(cos_t, jnp.float32)[:, None, :]
     sin_t = jnp.asarray(sin_t, jnp.float32)[:, None, :]
     twisted = jnp.concatenate([real * cos_t + imag * sin_t, imag * cos_t - real * sin_t], axis=-1)
-    cos_r, sin_r = angle_table(np.arange(rows), np.arange(rows), rows)
-    table = np.block([[cos_r, -sin_r], [sin_r, cos_r]])
-    spectrum = contract("rd,shkr->shkd", table, twisted)
+    spectrum = jnp.einsum("rd,shkr->shkd", table, twisted, precision=PRECISION)
     return spectrum[..., :rows], spectrum[..., rows:]
 
 
-def inverse(real, imag, padded):
+def inverse(real, imag, table, padded):
     _, half_count, _, rows = real.shape
     blocks = half_count - 1
     half = np.arange(half_count)
-    cos_r, sin_r = angle_table(np.arange(rows), np.arange(rows), rows)
-    table = np.block([[cos_r, sin_r], [-sin_r, cos_r]])
-    back = contract("dr,shkd->shkr", table, jnp.concatenate([real, imag], axis=-1))
+    back = jnp.einsum(
+        "rd,shkd->shkr", table, jnp.concatenate([real, imag], axis=-1), precision=PRECISION
+    )
     back_real, back_imag = back[..., :rows], back[..., rows:]
     cos_t, sin_t = angle_table(half, np.arange(rows), padded)
     cos_t = jnp.asarray(cos_t, jnp.float32)[:, None, :]
@@ -74,7 +81,8 @@
     stacked = jnp.stack([grad_conv, gated_value, long_filters[0], key_gate[0]])
     send = jnp.swapaxes(stacked, 1, 2).reshape(4, devices, group, rows)
     recv = lax.all_to_all(send, "seq", split_axis=1, concat_axis=1, tiled=True)
-    spec_real, spec_imag = forward(recv[:3].astype(jnp.float32), padded)
+    table = row_table(rows)
+    spec_real, spec_imag = forward(recv[:3].astype(jnp.float32), table, padded)
     conv_real, conv_imag = spec_real[0], spec_imag[0]
     gated_real, gated_imag = spec_real[1], spec_imag[1]
     filter_real, filter_imag = spec_real[2], spec_imag[2]
@@ -82,7 +90,7 @@
     back_imag = conv_imag * filter_real - conv_real * filter_imag
     fold_real = conv_real * gated_real + conv_imag * gated_imag
     fold_imag = conv_imag * gated_real - conv_real * gated_imag
-    both = inverse(jnp.stack([back_real, fold_real]), jnp.stack([back_imag, fold_imag]), padded)
+    both = inverse(jnp.stack([back_real, fold_real]), jnp.stack([back_imag, fold_imag]), table, padded)
     grad_gated, grad_filter = both[0], both[1]
     grad_value = recv[3].astype(jnp.float32) * grad_gated
     rim = jnp.concatenate(

time: 86.6 us -> 85 us (0.982)
  local copies, waits for them, and re-layouts: 10.7 us -> 9.25 us
  waiting for transfers between devices: 24.2 us -> 23.1 us
  other arithmetic: 3 us -> 4.04 us
    dot_general x0 -> x2, matrix products: none -> 6.05 us  [the longest x1 4.13 us: forward(): spectrum = jnp.einsum('rd,shkr->shkd', table, twisted, precision=PRECISION)]
    dot_general x4 -> x2, matrix products: 9.06 us -> 3.05 us  [contract(): jnp.einsum(form, jnp.asarray(table, jnp.float32), values, precision=PRECI...]
    unnamed x21 -> x17, local copies, waits for them, and re-layouts: 8.35 us -> 6.89 us
    all_to_all x1, waiting for transfers between devices: 24.1 us -> 23 us  [body(): recv = lax.all_to_all(send, 'seq', split_axis=1, concat_axis=1, tiled=True)]
    neg x0 -> x1, other arithmetic: none -> 1.1 us  [row_table(): -sin_r]
  transfers between devices with their start and end apart: 2 -> 2, of which waited for: 2 -> 2; matrix products, arithmetic and copies ran while one was open for 2% -> 3% of each run, Pallas kernels for 0% -> 0%
where the time goes in v6:
time: 85 us; the launch traced here: 84.6 us
  waiting for transfers between devices  23.1 us (27%)
  blocking collectives  22.1 us (26%)
  starting transfers between devices  16.1 us (19%)
  local copies, waits for them, and re-layouts  9.25 us (11%)
  matrix products  9.1 us (11%)
  other arithmetic  4.04 us (5%)
  between operations  0.92 us (1%)
    all_to_all x1, waiting for transfers between devices, body(): recv = lax.all_to_all(send, 'seq', split_axis=1, concat_axis=1, tiled=True)  23 us
    all_to_all x1, blocking collectives, body(): lax.all_to_all(outgoing, 'seq', split_axis=1, concat_axis=1, tiled=True)  22.1 us
    all_to_all x1, starting transfers between devices, body(): recv = lax.all_to_all(send, 'seq', split_axis=1, concat_axis=1, tiled=True)  12 us
    unnamed x17, local copies, waits for them, and re-layouts  6.89 us
    dot_general x1, matrix products, forward(): spectrum = jnp.einsum('rd,shkr->shkd', table, twisted, precision=PRECISION)  4.13 us
    ppermute x1, starting transfers between devices, shifted(): return lax.ppermute(block, axis, route)  4.1 us
    dot_general x2, matrix products, contract(): jnp.einsum(form, jnp.asarray(table, jnp.float32), values, precision=PRECI...  3.05 us
    dot_general x1, matrix products, inverse(): jnp.einsum('rd,shkd->shkr', table, jnp.concatenate([real, imag], axis=-1)...  1.91 us
  transfers between devices with their start and end apart: 2, of which 2 were waited for; matrix products, arithmetic and copies ran while one was open for 3% of the time, Pallas kernels for 0%

profile of v6, /device:TPU:1, one launch (start us, length us, event | category | flops | bytes accessed | tf_op | source)
XLA Modules:
  0.0 84.6 jit_solution(11206335812053938631)
XLA Ops:
  0.6 1.1 %copy.31 = bf16[1,256,512]{1,2,0:T(8,128)(2,1)S(1)} copy(bf16[1,256,512]{2,1,0:T(8,128)(2,1)} %param.14) | data formatting | bytes 524288 | tf_op args[2]
  1.8 1.1 %copy.30 = bf16[1,256,512]{1,2,0:T(8,128)(2,1)S(1)} copy(bf16[1,256,512]{2,1,0:T(8,128)(2,1)} %param.12) | data formatting | bytes 524288 | tf_op args[0]
  2.9 1.1 %copy.32 = bf16[1,256,512]{1,2,0:T(8,128)(2,1)S(1)} copy(bf16[1,256,512]{2,1,0:T(8,128)(2,1)} %param.13) | data formatting | bytes 524288 | tf_op args[1]
  4.0 1.1 %copy.29 = bf16[1,256,512]{1,2,0:T(8,128)(2,1)S(1)} copy(bf16[1,256,512]{2,1,0:T(8,128)(2,1)} %param.15) | data formatting | bytes 524288 | tf_op args[3]
  5.5 1.1 %copy.35 = bf16[4,32,16,256]{3,2,0,1:T(8,128)(2,1)} copy(bf16[4,32,16,256]{3,2,1,0:T(8,128)(2,1)S(1)} %bitcast.47) | data formatting | bytes 2097152 | tf_op jit(solution)/shard_map/reshape | solution.py:82
  6.6 12.0 %all-to-all-start = ((bf16[4,32,16,256]{3,2,0,1:T(8,128)(2,1)}), bf16[4,32,16,256]{3,2,0,1:T(8,128)(2,1)S(1)}, u32[]{:S(2)}, u32[]{:S(2)}) async-start(bf16[4,32,16,256]{3,2,0,1:T(8,128)(2,1)} %copy.35), calls=%async_computation | async-start | bytes 2097152 | tf_op jit(solution)/shard_map/all_to_all | solution.py:83
  18.6 0.8 fusion.28
  19.4 1.1 %fusion.26 = (f32[256,256]{1,0:T(8,128)S(1)}, f32[256,256]{1,0:T(8,128)S(1)}, f32[256,256]{1,0:T(8,128)S(1)}) fusion(s32[256]{0:T(256)S(1)} %iota.3), kind=kLoop, calls=%fused_computation.52 | loop fusion | flops 983040 | bytes 787456 | tf_op jit(solution)/shard_map/neg | solution.py:33
  20.5 23.0 %all-to-all-done = bf16[4,32,16,256]{3,2,0,1:T(8,128)(2,1)S(1)} async-done(((bf16[4,32,16,256]{3,2,0,1:T(8,128)(2,1)}), bf16[4,32,16,256]{3,2,0,1:T(8,128)(2,1)S(1)}, u32[]{:S(2)}, u32[]{:S(2)}) %all-to-all-start) | async-done | bytes 1048608 | tf_op jit(solution)/shard_map/all_to_all | solution.py:83
  43.6 1.1 %convolution_bitcast_fusion = f32[3,66,16,256]{3,1,2,0:T(8,128)S(1)} fusion(f32[66,32,1,1]{0,1,3,2:T(8,128)S(1)} %copy-done.4, bf16[3,32,16,256]{3,2,0,1:T(8,128)(2,1)S(1)} %slice.101), kind=kOutput, calls=%fused_computation.14 | convolution fusion | flops 155713536 | bytes 4038912 | tf_op jit(solution)/shard_map/ja,sakr->sjkr/dot_general | solution.py:25
  44.7 0.5 multiply_add_fusion
  45.3 0.6 pad_maximum_fusion
  45.9 4.1 %fusion = f32[3,33,16,512]{3,2,1,0:T(8,128)S(1)} fusion(f32[3,33,16,512]{3,1,2,0:T(8,128)S(1)} %pad_maximum_fusion, f32[256,256]{1,0:T(8,128)S(1)} %get-tuple-element.21, f32[256,256]{1,0:T(8,128)S(1)} %get-tuple-element.20, f32[256,256]{1,0:T(8,128)S(1)} %get-tuple-element.19), kind=kOutput, calls=%fused_computation.1 | convolution fusion | flops 2492203008 | bytes 7274496 | tf_op jit(solution)/shard_map/rd,shkr->shkd/dot_general | solution.py:47
  50.0 0.3 multiply_add_fusion.3
  50.3 1.9 %fusion.4 = f32[2,33,16,512]{3,2,1,0:T(8,128)S(1)} fusion(f32[1,33,16,256]{3,2,1,0:T(8,128)S(1)} %get-tuple-element.11, f32[1,33,16,256]{3,2,1,0:T(8,128)S(1)} %get-tuple-element.10, f32[1,33,16,256]{3,2,1,0:T(8,128)S(1)} %get-tuple-element.9, f32[1,33,16,256]{3,2,1,0:T(8,128)S(1)} %get-tuple-element.8, f32[256,256]{1,0:T(8,128)S(1)} %get-tuple-element.21, ...), kind=kOutput, calls=%fused_computation.5 | convolution fusion | flops 1663352832 | bytes 5111808 | tf_op jit(solution)/shard_map/rd,shkd->shkr/dot_general | solution.py:55
  52.2 0.3 multiply_subtract_fusion.1
  52.8 0.5 copy-done.3
  53.3 1.9 %fusion.12 = f32[2,32,16,256]{3,1,2,0:T(8,128)S(1)} fusion(f32[32,66,1,1]{1,0,3,2:T(8,128)S(1)} %copy-done.3, f32[2,66,16,256]{3,2,1,0:T(8,128)S(1)} %pad_maximum_fusion.1), kind=kOutput, calls=%fused_computation.17 | convolution fusion | flops 103809024 | bytes 3219712 | tf_op jit(solution)/shard_map/ac,sckr->sakr/dot_general | solution.py:25
  55.6 0.4 fusion.23
  56.0 0.3 copy.40
  56.3 22.1 %all_to_all.10 = bf16[2,32,16,256]{3,2,0,1:T(8,128)(2,1)S(1)} all-to-all(bf16[2,32,16,256]{3,2,0,1:T(8,128)(2,1)S(1)} %copy.40), channel_id=1, replica_groups=mesh['pipe'=2,'seq'=32,'chan'=4] {'seq'}, dimensions={1} | all-to-all | bytes 1048576 | tf_op jit(solution)/shard_map/all_to_all | solution.py:108
  78.5 4.1 %collective-permute-start = (bf16[1,256,512]{1,2,0:T(8,128)(2,1)S(1)}, bf16[1,256,512]{1,2,0:T(8,128)(2,1)S(1)}, u32[]{:S(2)}, u32[]{:S(2)}) collective-permute-start(bf16[1,256,512]{1,2,0:T(8,128)(2,1)S(1)} %bitcast.48), channel_id=1, source_target_pairs={{128,0},{0,128},{129,1},{1,129},{130,2},{2,130},{131,3},{3,131},{1... | collective-permute-start | bytes 786440 | tf_op jit(solution)/shard_map/ppermute | solution.py:16
  82.6 1.0 %copy.44 = f32[1,256,512]{2,1,0:T(8,128)} copy(f32[1,256,512]{1,2,0:T(8,128)S(1)} %convert_bitcast_fusion) | data formatting | bytes 1048576
  83.8 0.8 copy.43
  (24 shorter events, 1.2 us)
Async XLA Ops:
  0.6 4.4 %copy-start = (bf16[1,256,512]{2,1,0:T(8,128)(2,1)S(1)}, bf16[1,256,512]{2,1,0:T(8,128)(2,1)}, u32[]{:S(2)}) copy-start(bf16[1,256,512]{2,1,0:T(8,128)(2,1)} %param.17) | copy-start | bytes 786436
  6.6 36.9 %copy-start.4 = (f32[66,32,1,1]{0,1,3,2:T(8,128)S(1)}, f32[66,32,1,1]{0,1,3,2:T(8,128)}, u32[]{:S(2)}) copy-start(f32[66,32,1,1]{0,1,3,2:T(8,128)} %constant.51) | copy-start | bytes 25348
  6.6 36.9 %all-to-all-start = ((bf16[4,32,16,256]{3,2,0,1:T(8,128)(2,1)}), bf16[4,32,16,256]{3,2,0,1:T(8,128)(2,1)S(1)}, u32[]{:S(2)}, u32[]{:S(2)}) async-start(bf16[4,32,16,256]{3,2,0,1:T(8,128)(2,1)} %copy.35), calls=%async_computation | async-start | bytes 2097152 | tf_op jit(solution)/shard_map/all_to_all | solution.py:83
  43.5 1.2 %copy-start.1 = (f32[33,256]{1,0:T(8,128)S(1)}, f32[33,256]{1,0:T(8,128)}, u32[]{:S(2)}) copy-start(f32[33,256]{1,0:T(8,128)} %constant.41.clone) | copy-start | bytes 101380
  43.5 1.2 %copy-start.2 = (f32[33,256]{1,0:T(8,128)S(1)}, f32[33,256]{1,0:T(8,128)}, u32[]{:S(2)}) copy-start(f32[33,256]{1,0:T(8,128)} %constant.40.clone) | copy-start | bytes 101380
  52.6 0.7 copy-start.3
  78.5 5.3 %collective-permute-start = (bf16[1,256,512]{1,2,0:T(8,128)(2,1)S(1)}, bf16[1,256,512]{1,2,0:T(8,128)(2,1)S(1)}, u32[]{:S(2)}, u32[]{:S(2)}) collective-permute-start(bf16[1,256,512]{1,2,0:T(8,128)(2,1)S(1)} %bitcast.48), channel_id=1, source_target_pairs={{128,0},{0,128},{129,1},{1,129},{130,2},{2,130},{131,3},{3,131},{1... | collective-permute-start | bytes 786440 | tf_op jit(solution)/shard_map/ppermute | solution.py:16

commit v7 on v6

--- a/solution.py
+++ b/solution.py
@@ -17,8 +17,10 @@
 
 
 def angle_table(first, second, modulus):
-    angles = (np.outer(first, second) % modulus) * (2.0 * math.pi / modulus)
-    return np.cos(angles), np.sin(angles)
+    first = lax.optimization_barrier(jnp.asarray(first, jnp.int32))
+    products = (first[:, None] * jnp.asarray(second, jnp.int32)[None, :]) % modulus
+    angles = products.astype(jnp.float32) * (2.0 * math.pi / modulus)
+    return jnp.cos(angles), jnp.sin(angles)
 
 
 def contract(form, table, values):
@@ -38,11 +40,11 @@
     _, blocks, _, rows = signals.shape
     half = np.arange(blocks + 1)
     cos_b, sin_b = angle_table(half, np.arange(blocks), 2 * blocks)
-    first = contract("ja,sakr->sjkr", np.concatenate([cos_b, -sin_b]), signals)
+    first = contract("ja,sakr->sjkr", jnp.concatenate([cos_b, -sin_b]), signals)
     real, imag = first[:, : blocks + 1], first[:, blocks + 1 :]
     cos_t, sin_t = angle_table(half, np.arange(rows), padded)
-    cos_t = jnp.asarray(cos_t, jnp.float32)[:, None, :]
-    sin_t = jnp.asarray(sin_t, jnp.float32)[:, None, :]
+    cos_t = cos_t[:, None, :]
+    sin_t = sin_t[:, None, :]
     twisted = jnp.concatenate([real * cos_t + imag * sin_t, imag * cos_t - real * sin_t], axis=-1)
     spectrum = jnp.einsum("rd,shkr->shkd", table, twisted, precision=PRECISION)
     return spectrum[..., :rows], spectrum[..., rows:]
@@ -57,8 +59,8 @@
     )
     back_real, back_imag = back[..., :rows], back[..., rows:]
     cos_t, sin_t = angle_table(half, np.arange(rows), padded)
-    cos_t = jnp.asarray(cos_t, jnp.float32)[:, None, :]
-    sin_t = jnp.asarray(sin_t, jnp.float32)[:, None, :]
+    cos_t = cos_t[:, None, :]
+    sin_t = sin_t[:, None, :]
     twisted = jnp.concatenate(
         [back_real * cos_t - back_imag * sin_t, back_imag * cos_t + back_real * sin_t], axis=1
     )
@@ -66,7 +68,7 @@
     weight[0] = 1.0
     weight[blocks] = 1.0
     cos_b, sin_b = angle_table(np.arange(blocks), half, 2 * blocks)
-    table_b = np.concatenate([cos_b, -sin_b], axis=1) * np.concatenate([weight, weight])[None, :] / padded
+    table_b = jnp.concatenate([cos_b, -sin_b], axis=1) * jnp.asarray(np.concatenate([weight, weight]) / padded, jnp.float32)[None, :]
     return contract("ac,sckr->sakr", table_b, twisted)
 
 

time: 85 us -> 84.8 us (level)
    unnamed x17 -> x11, local copies, waits for them, and re-layouts: 6.89 us -> 6.81 us
  transfers between devices with their start and end apart: 2 -> 2, of which waited for: 2 -> 2; matrix products, arithmetic and copies ran while one was open for 3% -> 4% of each run, Pallas kernels for 0% -> 0%
where the time goes in v7:
time: 84.8 us; the launch traced here: 84.5 us
  waiting for transfers between devices  22.6 us (27%)
  blocking collectives  22.1 us (26%)
  starting transfers between devices  16 us (19%)
  local copies, waits for them, and re-layouts  9.18 us (11%)
  matrix products  9.18 us (11%)
  other arithmetic  4.56 us (5%)
  between operations  0.9 us (1%)
    all_to_all x1, waiting for transfers between devices, body(): recv = lax.all_to_all(send, 'seq', split_axis=1, concat_axis=1, tiled=True)  22.5 us
    all_to_all x1, blocking collectives, body(): lax.all_to_all(outgoing, 'seq', split_axis=1, concat_axis=1, tiled=True)  22.1 us
    all_to_all x1, starting transfers between devices, body(): recv = lax.all_to_all(send, 'seq', split_axis=1, concat_axis=1, tiled=True)  11.9 us
    unnamed x11, local copies, waits for them, and re-layouts  6.81 us
    dot_general x1, matrix products, forward(): spectrum = jnp.einsum('rd,shkr->shkd', table, twisted, precision=PRECISION)  4.13 us
    ppermute x1, starting transfers between devices, shifted(): return lax.ppermute(block, axis, route)  4.11 us
    dot_general x2, matrix products, contract(): jnp.einsum(form, jnp.asarray(table, jnp.float32), values, precision=PRECI...  3.13 us
    dot_general x1, matrix products, inverse(): jnp.einsum('rd,shkd->shkr', table, jnp.concatenate([real, imag], axis=-1)...  1.91 us
  transfers between devices with their start and end apart: 2, of which 2 were waited for; matrix products, arithmetic and copies ran while one was open for 4% of the time, Pallas kernels for 0%

profile of v7, /device:TPU:1, one launch (start us, length us, event | category | flops | bytes accessed | tf_op | source)
XLA Modules:
  0.0 84.5 jit_solution(11422781345467566795)
XLA Ops:
  0.6 1.1 %copy.34 = bf16[1,256,512]{1,2,0:T(8,128)(2,1)S(1)} copy(bf16[1,256,512]{2,1,0:T(8,128)(2,1)} %param.17) | data formatting | bytes 524288 | tf_op args[2]
  1.8 1.1 %copy.33 = bf16[1,256,512]{1,2,0:T(8,128)(2,1)S(1)} copy(bf16[1,256,512]{2,1,0:T(8,128)(2,1)} %param.15) | data formatting | bytes 524288 | tf_op args[0]
  2.9 1.1 %copy.35 = bf16[1,256,512]{1,2,0:T(8,128)(2,1)S(1)} copy(bf16[1,256,512]{2,1,0:T(8,128)(2,1)} %param.16) | data formatting | bytes 524288 | tf_op args[1]
  4.0 1.1 %copy.32 = bf16[1,256,512]{1,2,0:T(8,128)(2,1)S(1)} copy(bf16[1,256,512]{2,1,0:T(8,128)(2,1)} %param.18) | data formatting | bytes 524288 | tf_op args[3]
  5.5 1.1 %copy.38 = bf16[4,32,16,256]{3,2,0,1:T(8,128)(2,1)} copy(bf16[4,32,16,256]{3,2,1,0:T(8,128)(2,1)S(1)} %bitcast.49) | data formatting | bytes 2097152 | tf_op jit(solution)/shard_map/reshape | solution.py:84
  6.6 11.9 %all-to-all-start = ((bf16[4,32,16,256]{3,2,0,1:T(8,128)(2,1)}), bf16[4,32,16,256]{3,2,0,1:T(8,128)(2,1)S(1)}, u32[]{:S(2)}, u32[]{:S(2)}) async-start(bf16[4,32,16,256]{3,2,0,1:T(8,128)(2,1)} %copy.38), calls=%async_computation | async-start | bytes 2097152 | tf_op jit(solution)/shard_map/all_to_all | solution.py:85
  18.5 0.8 fusion.57
  19.8 1.1 %fusion.26 = (f32[256,256]{1,0:T(8,128)S(1)}, f32[256,256]{1,0:T(8,128)S(1)}, f32[256,256]{1,0:T(8,128)S(1)}) fusion(s32[256]{0:T(256)S(1)} %iota.6), kind=kLoop, calls=%fused_computation.52 | loop fusion | flops 983040 | bytes 787456 | tf_op jit(solution)/shard_map/neg | solution.py:35
  20.9 22.5 %all-to-all-done = bf16[4,32,16,256]{3,2,0,1:T(8,128)(2,1)S(1)} async-done(((bf16[4,32,16,256]{3,2,0,1:T(8,128)(2,1)}), bf16[4,32,16,256]{3,2,0,1:T(8,128)(2,1)S(1)}, u32[]{:S(2)}, u32[]{:S(2)}) %all-to-all-start) | async-done | bytes 1048608 | tf_op jit(solution)/shard_map/all_to_all | solution.py:85
  43.4 1.2 %convolution_bitcast_fusion = f32[3,66,16,256]{3,1,2,0:T(8,128)S(1)} fusion(bf16[3,32,16,256]{3,2,0,1:T(8,128)(2,1)S(1)} %slice.101, f32[33,32]{0,1:T(8,128)S(1)} %get-tuple-element.27, f32[33,32]{0,1:T(8,128)S(1)} %get-tuple-element.26), kind=kOutput, calls=%fused_computation.14 | convolution fusion | flops 155715648 | bytes 4038912 | tf_op jit(solution)/shard_map/ja,sakr->sjkr/dot_general | solution.py:27
  44.6 0.5 multiply_add_fusion
  45.2 0.6 pad_maximum_fusion
  45.8 4.1 %fusion = f32[3,33,16,512]{3,2,1,0:T(8,128)S(1)} fusion(f32[3,33,16,512]{3,1,2,0:T(8,128)S(1)} %pad_maximum_fusion, f32[256,256]{1,0:T(8,128)S(1)} %get-tuple-element.21, f32[256,256]{1,0:T(8,128)S(1)} %get-tuple-element.20, f32[256,256]{1,0:T(8,128)S(1)} %get-tuple-element.19), kind=kOutput, calls=%fused_computation.1 | convolution fusion | flops 2492203008 | bytes 7274496 | tf_op jit(solution)/shard_map/rd,shkr->shkd/dot_general | solution.py:49
  49.9 0.3 multiply_add_fusion.3
  50.2 1.9 %fusion.4 = f32[2,33,16,512]{3,2,1,0:T(8,128)S(1)} fusion(f32[1,33,16,256]{3,2,1,0:T(8,128)S(1)} %get-tuple-element.11, f32[1,33,16,256]{3,2,1,0:T(8,128)S(1)} %get-tuple-element.10, f32[1,33,16,256]{3,2,1,0:T(8,128)S(1)} %get-tuple-element.9, f32[1,33,16,256]{3,2,1,0:T(8,128)S(1)} %get-tuple-element.8, f32[256,256]{1,0:T(8,128)S(1)} %get-tuple-element.21, ...), kind=kOutput, calls=%fused_computation.5 | convolution fusion | flops 1663352832 | bytes 5111808 | tf_op jit(solution)/shard_map/rd,shkd->shkr/dot_general | solution.py:57
  52.1 0.4 multiply_subtract_fusion.1
  52.7 0.5 copy-done.1
  53.2 1.9 %fusion.12 = f32[2,32,16,256]{3,1,2,0:T(8,128)S(1)} fusion(f32[2,66,16,256]{3,2,1,0:T(8,128)S(1)} %pad_maximum_fusion.1, f32[32,33]{1,0:T(8,128)S(1)} %get-tuple-element.23, f32[32,33]{1,0:T(8,128)S(1)} %get-tuple-element.22, f32[66]{0:T(128)S(1)} %copy-done.1), kind=kOutput, calls=%fused_computation.17 | convolution fusion | flops 103813248 | bytes 3219976 | tf_op jit(solution)/shard_map/ac,sckr->sakr/dot_general | solution.py:27
  55.4 0.4 fusion.23
  55.9 0.3 copy.43
  56.2 22.1 %all_to_all.10 = bf16[2,32,16,256]{3,2,0,1:T(8,128)(2,1)S(1)} all-to-all(bf16[2,32,16,256]{3,2,0,1:T(8,128)(2,1)S(1)} %copy.43), channel_id=1, replica_groups=mesh['pipe'=2,'seq'=32,'chan'=4] {'seq'}, dimensions={1} | all-to-all | bytes 1048576 | tf_op jit(solution)/shard_map/all_to_all | solution.py:110
  78.3 4.1 %collective-permute-start = (bf16[1,256,512]{1,2,0:T(8,128)(2,1)S(1)}, bf16[1,256,512]{1,2,0:T(8,128)(2,1)S(1)}, u32[]{:S(2)}, u32[]{:S(2)}) collective-permute-start(bf16[1,256,512]{1,2,0:T(8,128)(2,1)S(1)} %bitcast.50), channel_id=1, source_target_pairs={{128,0},{0,128},{129,1},{1,129},{130,2},{2,130},{131,3},{3,131},{1... | collective-permute-start | bytes 786440 | tf_op jit(solution)/shard_map/ppermute | solution.py:16
  82.5 1.0 %copy.47 = f32[1,256,512]{2,1,0:T(8,128)} copy(f32[1,256,512]{1,2,0:T(8,128)S(1)} %convert_bitcast_fusion) | data formatting | bytes 1048576
  83.6 0.8 copy.46
  (23 shorter events, 1.7 us)
Async XLA Ops:
  0.6 4.4 %copy-start = (bf16[1,256,512]{2,1,0:T(8,128)(2,1)S(1)}, bf16[1,256,512]{2,1,0:T(8,128)(2,1)}, u32[]{:S(2)}) copy-start(bf16[1,256,512]{2,1,0:T(8,128)(2,1)} %param.20) | copy-start | bytes 786436
  6.6 36.7 %all-to-all-start = ((bf16[4,32,16,256]{3,2,0,1:T(8,128)(2,1)}), bf16[4,32,16,256]{3,2,0,1:T(8,128)(2,1)S(1)}, u32[]{:S(2)}, u32[]{:S(2)}) async-start(bf16[4,32,16,256]{3,2,0,1:T(8,128)(2,1)} %copy.38), calls=%async_computation | async-start | bytes 2097152 | tf_op jit(solution)/shard_map/all_to_all | solution.py:85
  52.5 0.7 copy-start.1
  78.3 5.3 %collective-permute-start = (bf16[1,256,512]{1,2,0:T(8,128)(2,1)S(1)}, bf16[1,256,512]{1,2,0:T(8,128)(2,1)S(1)}, u32[]{:S(2)}, u32[]{:S(2)}) collective-permute-start(bf16[1,256,512]{1,2,0:T(8,128)(2,1)S(1)} %bitcast.50), channel_id=1, source_target_pairs={{128,0},{0,128},{129,1},{1,129},{130,2},{2,130},{131,3},{3,131},{1... | collective-permute-start | bytes 786440 | tf_op jit(solution)/shard_map/ppermute | solution.py:16

commit v8 on v7

--- a/solution.py
+++ b/solution.py
@@ -5,6 +5,7 @@
 import jax
 import jax.numpy as jnp
 from jax import lax
+from jax.experimental import pallas as pl
 from jax.sharding import PartitionSpec as P
 
 PRECISION = lax.Precision.HIGH
@@ -72,19 +73,28 @@
     return contract("ac,sckr->sakr", table_b, twisted)
 
 
+def prep_kernel(grad_ref, value_ref, key_ref, query_ref, filter_ref, out_ref):
+    key = key_ref[...].astype(jnp.float32)
+    grad_conv = (query_ref[...].astype(jnp.float32) * grad_ref[...].astype(jnp.float32)).astype(jnp.bfloat16)
+    gated_value = (key * value_ref[...].astype(jnp.float32)).astype(jnp.bfloat16)
+    devices, _, group, rows = out_ref.shape
+    for index, block in enumerate([grad_conv, gated_value, filter_ref[...], key_ref[...]]):
+        flipped = block.astype(jnp.float32).T.reshape(devices, group, rows)
+        out_ref[:, index] = flipped.astype(jnp.bfloat16)
+
+
 def body(grad_out, value_branch, key_gate, query_gate, short_weights, long_filters):
     rows, columns = grad_out.shape[1:]
     devices = lax.axis_size("seq")
     position = lax.axis_index("seq")
     group = columns // devices
     padded = 2 * rows * devices
-    grad_conv = (query_gate[0].astype(jnp.float32) * grad_out[0].astype(jnp.float32)).astype(jnp.bfloat16)
-    gated_value = (key_gate[0].astype(jnp.float32) * value_branch[0].astype(jnp.float32)).astype(jnp.bfloat16)
-    stacked = jnp.stack([grad_conv, gated_value, long_filters[0], key_gate[0]])
-    send = jnp.swapaxes(stacked, 1, 2).reshape(4, devices, group, rows)
-    recv = lax.all_to_all(send, "seq", split_axis=1, concat_axis=1, tiled=True)
+    send = pl.pallas_call(
+        prep_kernel, out_shape=jax.ShapeDtypeStruct((devices, 4, group, rows), jnp.bfloat16)
+    )(grad_out[0], value_branch[0], key_gate[0], query_gate[0], long_filters[0])
+    recv = lax.all_to_all(send, "seq", split_axis=0, concat_axis=0, tiled=True)
     table = row_table(rows)
-    spec_real, spec_imag = forward(recv[:3].astype(jnp.float32), table, padded)
+    spec_real, spec_imag = forward(jnp.swapaxes(recv[:, :3], 0, 1).astype(jnp.float32), table, padded)
     conv_real, conv_imag = spec_real[0], spec_imag[0]
     gated_real, gated_imag = spec_real[1], spec_imag[1]
     filter_real, filter_imag = spec_real[2], spec_imag[2]
@@ -94,7 +104,7 @@
     fold_imag = conv_imag * gated_real - conv_real * gated_imag
     both = inverse(jnp.stack([back_real, fold_real]), jnp.stack([back_imag, fold_imag]), table, padded)
     grad_gated, grad_filter = both[0], both[1]
-    grad_value = recv[3].astype(jnp.float32) * grad_gated
+    grad_value = recv[:, 3].astype(jnp.float32) * grad_gated
     rim = jnp.concatenate(
         [grad_value[1:, :, :2], jnp.zeros((1, group, 2), grad_value.dtype)], axis=0
     )

time: 84.8 us -> 81.8 us (0.965)
  local copies, waits for them, and re-layouts: 9.18 us -> 4.07 us
  Pallas kernels: 0 us -> 2.61 us
    unnamed x11 -> x3, local copies, waits for them, and re-layouts: 6.81 us -> 1.16 us
    pallas_call x0 -> x1, Pallas kernels: none -> 2.61 us  [body(): pl.pallas_call(prep_kernel, out_shape=jax.ShapeDtypeStruct((devices, 4, g...]
    reshape x1 -> x0, local copies, waits for them, and re-layouts: 1.12 us -> none  [body(): send = jnp.swapaxes(stacked, 1, 2).reshape(4, devices, group, rows)]
    broadcast_in_dim x0 -> x1, local copies, waits for them, and re-layouts: none -> 1 us  [body(): return (passed, filter_tokens[None])]
where the time goes in v8:
time: 81.8 us; the launch traced here: 81.5 us
  waiting for transfers between devices  22.6 us (28%)
  blocking collectives  22.1 us (27%)
  starting transfers between devices  16 us (20%)
  matrix products  9.18 us (11%)
  other arithmetic  4.18 us (5%)
  local copies, waits for them, and re-layouts  4.07 us (5%)
  Pallas kernels  2.61 us (3%)
  between operations  0.85 us (1%)
    all_to_all x1, waiting for transfers between devices, body(): recv = lax.all_to_all(send, 'seq', split_axis=0, concat_axis=0, tiled=True)  22.4 us
    all_to_all x1, blocking collectives, body(): lax.all_to_all(outgoing, 'seq', split_axis=1, concat_axis=1, tiled=True)  22.1 us
    all_to_all x1, starting transfers between devices, body(): recv = lax.all_to_all(send, 'seq', split_axis=0, concat_axis=0, tiled=True)  11.9 us
    dot_general x1, matrix products, forward(): spectrum = jnp.einsum('rd,shkr->shkd', table, twisted, precision=PRECISION)  4.13 us
    ppermute x1, starting transfers between devices, shifted(): return lax.ppermute(block, axis, route)  4.1 us
    dot_general x2, matrix products, contract(): jnp.einsum(form, jnp.asarray(table, jnp.float32), values, precision=PRECI...  3.13 us
    pallas_call x1, Pallas kernels, body(): pl.pallas_call(prep_kernel, out_shape=jax.ShapeDtypeStruct((devices, 4, g...  2.61 us
    dot_general x1, matrix products, inverse(): jnp.einsum('rd,shkd->shkr', table, jnp.concatenate([real, imag], axis=-1)...  1.92 us
  transfers between devices with their start and end apart: 2, of which 2 were waited for; matrix products, arithmetic and copies ran while one was open for 4% of the time, Pallas kernels for 0%

profile of v8, /device:TPU:1, one launch (start us, length us, event | category | flops | bytes accessed | tf_op | source)
XLA Modules:
  0.0 81.5 jit_solution(1186290413266215431)
XLA Ops:
  0.6 2.6 %shard_map.158 = bf16[32,4,16,256]{3,2,1,0:T(8,128)(2,1)} custom-call(bf16[256,512]{1,0:T(8,128)(2,1)} %bitcast.59, bf16[256,512]{1,0:T(8,128)(2,1)} %bitcast.60, bf16[256,512]{1,0:T(8,128)(2,1)} %bitcast.61, bf16[256,512]{1,0:T(8,128)(2,1)} %bitcast.62, bf16[256,512]{1,0:T(8,128)(2,1)} %bitcast.63), custom_call_target="tpu_custom_call" | custom-call | tf_op jit(solution)/shard_map/pallas_call | solution.py:92
  3.2 11.9 %all-to-all-start = ((bf16[32,4,16,256]{3,2,1,0:T(8,128)(2,1)}), bf16[32,4,16,256]{3,2,1,0:T(8,128)(2,1)S(1)}, u32[]{:S(2)}, u32[]{:S(2)}) async-start(bf16[32,4,16,256]{3,2,1,0:T(8,128)(2,1)} %shard_map.158), calls=%async_computation | async-start | bytes 2097152 | tf_op jit(solution)/shard_map/all_to_all | solution.py:95
  15.1 0.8 fusion.54
  16.0 0.2 fusion.51
  16.2 0.2 fusion.31
  16.4 1.1 %fusion.23 = (f32[256,256]{1,0:T(8,128)S(1)}, f32[256,256]{1,0:T(8,128)S(1)}, f32[256,256]{1,0:T(8,128)S(1)}) fusion(s32[256]{0:T(256)S(1)} %iota.6), kind=kLoop, calls=%fused_computation.51 | loop fusion | flops 983040 | bytes 787456 | tf_op jit(solution)/shard_map/neg | solution.py:36
  17.5 22.4 %all-to-all-done = bf16[32,4,16,256]{3,2,1,0:T(8,128)(2,1)S(1)} async-done(((bf16[32,4,16,256]{3,2,1,0:T(8,128)(2,1)}), bf16[32,4,16,256]{3,2,1,0:T(8,128)(2,1)S(1)}, u32[]{:S(2)}, u32[]{:S(2)}) %all-to-all-start) | async-done | bytes 1048608 | tf_op jit(solution)/shard_map/all_to_all | solution.py:95
  40.0 1.2 %convolution_bitcast_fusion = f32[3,66,16,256]{3,1,2,0:T(8,128)S(1)} fusion(bf16[3,32,16,256]{3,2,0,1:T(8,128)(2,1)S(1)} %slice_bitcast_fusion, f32[33,32]{0,1:T(8,128)S(1)} %get-tuple-element.23, f32[33,32]{0,1:T(8,128)S(1)} %get-tuple-element.22), kind=kOutput, calls=%fused_computation.14 | convolution fusion | flops 155715648 | bytes 4038912 | tf_op jit(solution)/shard_map/ja,sakr->sjkr/dot_general | solution.py:28
  41.2 0.5 multiply_add_fusion
  41.8 0.6 pad_maximum_fusion
  42.4 4.1 %fusion = f32[3,33,16,512]{3,2,1,0:T(8,128)S(1)} fusion(f32[3,33,16,512]{3,1,2,0:T(8,128)S(1)} %pad_maximum_fusion, f32[256,256]{1,0:T(8,128)S(1)} %get-tuple-element.17, f32[256,256]{1,0:T(8,128)S(1)} %get-tuple-element.16, f32[256,256]{1,0:T(8,128)S(1)} %get-tuple-element.15), kind=kOutput, calls=%fused_computation.1 | convolution fusion | flops 2492203008 | bytes 7274496 | tf_op jit(solution)/shard_map/rd,shkr->shkd/dot_general | solution.py:50
  46.5 0.3 multiply_add_fusion.3
  46.9 1.9 %fusion.4 = f32[2,33,16,512]{3,2,1,0:T(8,128)S(1)} fusion(f32[1,33,16,256]{3,2,1,0:T(8,128)S(1)} %get-tuple-element.7, f32[1,33,16,256]{3,2,1,0:T(8,128)S(1)} %get-tuple-element.6, f32[1,33,16,256]{3,2,1,0:T(8,128)S(1)} %get-tuple-element.5, f32[1,33,16,256]{3,2,1,0:T(8,128)S(1)} %get-tuple-element.4, f32[256,256]{1,0:T(8,128)S(1)} %get-tuple-element.17, ...), kind=kOutput, calls=%fused_computation.5 | convolution fusion | flops 1663352832 | bytes 5111808 | tf_op jit(solution)/shard_map/rd,shkd->shkr/dot_general | solution.py:58
  48.8 0.4 multiply_subtract_fusion.1
  49.2 0.2 pad_maximum_fusion.1
  49.3 0.5 copy-done
  49.8 1.9 %fusion.2 = f32[2,16,256,32]{2,3,1,0:T(8,128)S(1)} fusion(f32[2,66,16,256]{3,2,1,0:T(8,128)S(1)} %pad_maximum_fusion.1, f32[32,33]{1,0:T(8,128)S(1)} %get-tuple-element.19, f32[32,33]{1,0:T(8,128)S(1)} %get-tuple-element.18, f32[66]{0:T(128)S(1)} %copy-done), kind=kOutput, calls=%fused_computation.3 | convolution fusion | flops 103813248 | bytes 3219976 | tf_op jit(solution)/shard_map/ac,sckr->sakr/dot_general | solution.py:28
  51.7 0.8 copy.40
  52.8 0.4 fusion.20
  53.2 22.1 %all_to_all.10 = bf16[2,32,16,256]{3,2,0,1:T(8,128)(2,1)S(1)} all-to-all(bf16[2,32,16,256]{3,2,0,1:T(8,128)(2,1)S(1)} %copy.27), channel_id=1, replica_groups=mesh['pipe'=2,'seq'=32,'chan'=4] {'seq'}, dimensions={1} | all-to-all | bytes 1048576 | tf_op jit(solution)/shard_map/all_to_all | solution.py:120
  75.4 0.1 copy.28
  75.6 4.1 %collective-permute-start = (bf16[1,256,512]{2,1,0:T(8,128)(2,1)S(1)}, bf16[1,256,512]{2,1,0:T(8,128)(2,1)S(1)}, u32[]{:S(2)}, u32[]{:S(2)}) collective-permute-start(bf16[1,256,512]{2,1,0:T(8,128)(2,1)S(1)} %bitcast.64), channel_id=1, source_target_pairs={{128,0},{0,128},{129,1},{1,129},{130,2},{2,130},{131,3},{3,131},{1... | collective-permute-start | bytes 786440 | tf_op jit(solution)/shard_map/ppermute | solution.py:17
  79.7 1.0 %copy.29 = f32[512,256]{0,1:T(8,128)} copy(f32[512,256]{1,0:T(8,128)S(1)} %bitcast_convert_fusion) | data formatting | bytes 1048576 | tf_op jit(solution)/shard_map/broadcast_in_dim | solution.py:125
  80.8 0.7 copy.42
  (15 shorter events, 0.7 us)
Async XLA Ops:
  3.2 36.7 %all-to-all-start = ((bf16[32,4,16,256]{3,2,1,0:T(8,128)(2,1)}), bf16[32,4,16,256]{3,2,1,0:T(8,128)(2,1)S(1)}, u32[]{:S(2)}, u32[]{:S(2)}) async-start(bf16[32,4,16,256]{3,2,1,0:T(8,128)(2,1)} %shard_map.158), calls=%async_computation | async-start | bytes 2097152 | tf_op jit(solution)/shard_map/all_to_all | solution.py:95
  49.1 0.7 copy-start
  75.6 5.3 %collective-permute-start = (bf16[1,256,512]{2,1,0:T(8,128)(2,1)S(1)}, bf16[1,256,512]{2,1,0:T(8,128)(2,1)S(1)}, u32[]{:S(2)}, u32[]{:S(2)}) collective-permute-start(bf16[1,256,512]{2,1,0:T(8,128)(2,1)S(1)} %bitcast.64), channel_id=1, source_target_pairs={{128,0},{0,128},{129,1},{1,129},{130,2},{2,130},{131,3},{3,131},{1... | collective-permute-start | bytes 786440 | tf_op jit(solution)/shard_map/ppermute | solution.py:17

commit v9 on v8

--- a/solution.py
+++ b/solution.py
@@ -70,7 +70,7 @@
     weight[blocks] = 1.0
     cos_b, sin_b = angle_table(np.arange(blocks), half, 2 * blocks)
     table_b = jnp.concatenate([cos_b, -sin_b], axis=1) * jnp.asarray(np.concatenate([weight, weight]) / padded, jnp.float32)[None, :]
-    return contract("ac,sckr->sakr", table_b, twisted)
+    return contract("ac,sckr->askr", table_b, twisted)
 
 
 def prep_kernel(grad_ref, value_ref, key_ref, query_ref, filter_ref, out_ref):
@@ -103,7 +103,7 @@
     fold_real = conv_real * gated_real + conv_imag * gated_imag
     fold_imag = conv_imag * gated_real - conv_real * gated_imag
     both = inverse(jnp.stack([back_real, fold_real]), jnp.stack([back_imag, fold_imag]), table, padded)
-    grad_gated, grad_filter = both[0], both[1]
+    grad_gated, grad_filter = both[:, 0], both[:, 1]
     grad_value = recv[:, 3].astype(jnp.float32) * grad_gated
     rim = jnp.concatenate(
         [grad_value[1:, :, :2], jnp.zeros((1, group, 2), grad_value.dtype)], axis=0

time: 81.8 us -> 81.6 us (level)
  no operation moved by 1% of the time
where the time goes in v9:
time: 81.6 us; the launch traced here: 81.3 us
  waiting for transfers between devices  22.6 us (28%)
  blocking collectives  22.1 us (27%)
  starting transfers between devices  16 us (20%)
  matrix products  9.31 us (11%)
  other arithmetic  4.42 us (5%)
  local copies, waits for them, and re-layouts  3.46 us (4%)
  Pallas kernels  2.61 us (3%)
  between operations  0.85 us (1%)
    all_to_all x1, waiting for transfers between devices, body(): recv = lax.all_to_all(send, 'seq', split_axis=0, concat_axis=0, tiled=True)  22.4 us
    all_to_all x1, blocking collectives, body(): lax.all_to_all(outgoing, 'seq', split_axis=1, concat_axis=1, tiled=True)  22.1 us
    all_to_all x1, starting transfers between devices, body(): recv = lax.all_to_all(send, 'seq', split_axis=0, concat_axis=0, tiled=True)  11.9 us
    dot_general x1, matrix products, forward(): spectrum = jnp.einsum('rd,shkr->shkd', table, twisted, precision=PRECISION)  4.13 us
    ppermute x1, starting transfers between devices, shifted(): return lax.ppermute(block, axis, route)  4.1 us
    dot_general x2, matrix products, contract(): jnp.einsum(form, jnp.asarray(table, jnp.float32), values, precision=PRECI...  3.26 us
    pallas_call x1, Pallas kernels, body(): pl.pallas_call(prep_kernel, out_shape=jax.ShapeDtypeStruct((devices, 4, g...  2.61 us
    dot_general x1, matrix products, inverse(): jnp.einsum('rd,shkd->shkr', table, jnp.concatenate([real, imag], axis=-1)...  1.92 us
  transfers between devices with their start and end apart: 2, of which 2 were waited for; matrix products, arithmetic and copies ran while one was open for 4% of the time, Pallas kernels for 0%

profile of v9, /device:TPU:1, one launch (start us, length us, event | category | flops | bytes accessed | tf_op | source)
XLA Modules:
  0.0 81.3 jit_solution(15231459845372414933)
XLA Ops:
  0.6 2.6 %shard_map.158 = bf16[32,4,16,256]{3,2,1,0:T(8,128)(2,1)} custom-call(bf16[256,512]{1,0:T(8,128)(2,1)} %bitcast.51, bf16[256,512]{1,0:T(8,128)(2,1)} %bitcast.52, bf16[256,512]{1,0:T(8,128)(2,1)} %bitcast.53, bf16[256,512]{1,0:T(8,128)(2,1)} %bitcast.54, bf16[256,512]{1,0:T(8,128)(2,1)} %bitcast.55), custom_call_target="tpu_custom_call" | custom-call | tf_op jit(solution)/shard_map/pallas_call | solution.py:92
  3.2 11.9 %all-to-all-start = ((bf16[32,4,16,256]{3,2,1,0:T(8,128)(2,1)}), bf16[32,4,16,256]{3,2,1,0:T(8,128)(2,1)S(1)}, u32[]{:S(2)}, u32[]{:S(2)}) async-start(bf16[32,4,16,256]{3,2,1,0:T(8,128)(2,1)} %shard_map.158), calls=%async_computation | async-start | bytes 2097152 | tf_op jit(solution)/shard_map/all_to_all | solution.py:95
  15.1 0.8 fusion.55
  16.0 0.2 fusion.53
  16.2 0.2 fusion.32
  16.4 1.1 %fusion.24 = (f32[256,256]{1,0:T(8,128)S(1)}, f32[256,256]{1,0:T(8,128)S(1)}, f32[256,256]{1,0:T(8,128)S(1)}) fusion(s32[256]{0:T(256)S(1)} %iota.6), kind=kLoop, calls=%fused_computation.50 | loop fusion | flops 983040 | bytes 787456 | tf_op jit(solution)/shard_map/neg | solution.py:36
  17.5 22.4 %all-to-all-done = bf16[32,4,16,256]{3,2,1,0:T(8,128)(2,1)S(1)} async-done(((bf16[32,4,16,256]{3,2,1,0:T(8,128)(2,1)}), bf16[32,4,16,256]{3,2,1,0:T(8,128)(2,1)S(1)}, u32[]{:S(2)}, u32[]{:S(2)}) %all-to-all-start) | async-done | bytes 1048608 | tf_op jit(solution)/shard_map/all_to_all | solution.py:95
  40.0 1.2 %convolution_bitcast_fusion = f32[3,66,16,256]{3,1,2,0:T(8,128)S(1)} fusion(bf16[3,32,16,256]{3,2,0,1:T(8,128)(2,1)S(1)} %slice_bitcast_fusion, f32[33,32]{0,1:T(8,128)S(1)} %get-tuple-element.23, f32[33,32]{0,1:T(8,128)S(1)} %get-tuple-element.22), kind=kOutput, calls=%fused_computation.14 | convolution fusion | flops 155715648 | bytes 4038912 | tf_op jit(solution)/shard_map/ja,sakr->sjkr/dot_general | solution.py:28
  41.2 0.5 multiply_add_fusion
  41.8 0.6 pad_maximum_fusion
  42.4 4.1 %fusion = f32[3,33,16,512]{3,2,1,0:T(8,128)S(1)} fusion(f32[3,33,16,512]{3,1,2,0:T(8,128)S(1)} %pad_maximum_fusion, f32[256,256]{1,0:T(8,128)S(1)} %get-tuple-element.17, f32[256,256]{1,0:T(8,128)S(1)} %get-tuple-element.16, f32[256,256]{1,0:T(8,128)S(1)} %get-tuple-element.15), kind=kOutput, calls=%fused_computation.1 | convolution fusion | flops 2492203008 | bytes 7274496 | tf_op jit(solution)/shard_map/rd,shkr->shkd/dot_general | solution.py:50
  46.5 0.3 multiply_add_fusion.3
  46.9 1.9 %fusion.4 = f32[2,33,16,512]{3,2,1,0:T(8,128)S(1)} fusion(f32[1,33,16,256]{3,2,1,0:T(8,128)S(1)} %get-tuple-element.7, f32[1,33,16,256]{3,2,1,0:T(8,128)S(1)} %get-tuple-element.6, f32[1,33,16,256]{3,2,1,0:T(8,128)S(1)} %get-tuple-element.5, f32[1,33,16,256]{3,2,1,0:T(8,128)S(1)} %get-tuple-element.4, f32[256,256]{1,0:T(8,128)S(1)} %get-tuple-element.17, ...), kind=kOutput, calls=%fused_computation.5 | convolution fusion | flops 1663352832 | bytes 5111808 | tf_op jit(solution)/shard_map/rd,shkd->shkr/dot_general | solution.py:58
  48.8 0.4 multiply_subtract_fusion.1
  49.2 0.2 pad_maximum_fusion.1
  49.3 0.5 copy-done
  49.8 2.1 %fusion.2 = f32[32,2,16,256]{3,0,2,1:T(8,128)S(1)} fusion(f32[2,66,16,256]{3,2,1,0:T(8,128)S(1)} %pad_maximum_fusion.1, f32[32,33]{1,0:T(8,128)S(1)} %get-tuple-element.19, f32[32,33]{1,0:T(8,128)S(1)} %get-tuple-element.18, f32[66]{0:T(128)S(1)} %copy-done), kind=kOutput, calls=%fused_computation.3 | convolution fusion | flops 103813248 | bytes 3219976 | tf_op jit(solution)/shard_map/ac,sckr->askr/dot_general | solution.py:28
  52.0 0.3 fusion.16
  52.4 0.2 copy.49
  52.5 0.4 fusion.20
  53.0 22.1 %all_to_all.10 = bf16[2,32,16,256]{3,2,0,1:T(8,128)(2,1)S(1)} all-to-all(bf16[2,32,16,256]{3,2,0,1:T(8,128)(2,1)S(1)} %copy.29), channel_id=1, replica_groups=mesh['pipe'=2,'seq'=32,'chan'=4] {'seq'}, dimensions={1} | all-to-all | bytes 1048576 | tf_op jit(solution)/shard_map/all_to_all | solution.py:120
  75.3 4.1 %collective-permute-start = (bf16[1,256,512]{2,1,0:T(8,128)(2,1)S(1)}, bf16[1,256,512]{2,1,0:T(8,128)(2,1)S(1)}, u32[]{:S(2)}, u32[]{:S(2)}) collective-permute-start(bf16[1,256,512]{2,1,0:T(8,128)(2,1)S(1)} %bitcast.56), channel_id=1, source_target_pairs={{128,0},{0,128},{129,1},{1,129},{130,2},{2,130},{131,3},{3,131},{1... | collective-permute-start | bytes 786440 | tf_op jit(solution)/shard_map/ppermute | solution.py:17
  79.5 1.0 %copy.31 = f32[512,256]{0,1:T(8,128)} copy(f32[512,256]{1,0:T(8,128)S(1)} %bitcast_convert_fusion) | data formatting | bytes 1048576 | tf_op jit(solution)/shard_map/broadcast_in_dim | solution.py:125
  80.6 0.7 copy.51
  (16 shorter events, 0.7 us)
Async XLA Ops:
  3.2 36.7 %all-to-all-start = ((bf16[32,4,16,256]{3,2,1,0:T(8,128)(2,1)}), bf16[32,4,16,256]{3,2,1,0:T(8,128)(2,1)S(1)}, u32[]{:S(2)}, u32[]{:S(2)}) async-start(bf16[32,4,16,256]{3,2,1,0:T(8,128)(2,1)} %shard_map.158), calls=%async_computation | async-start | bytes 2097152 | tf_op jit(solution)/shard_map/all_to_all | solution.py:95
  49.1 0.7 copy-start
  75.3 5.3 %collective-permute-start = (bf16[1,256,512]{2,1,0:T(8,128)(2,1)S(1)}, bf16[1,256,512]{2,1,0:T(8,128)(2,1)S(1)}, u32[]{:S(2)}, u32[]{:S(2)}) collective-permute-start(bf16[1,256,512]{2,1,0:T(8,128)(2,1)S(1)} %bitcast.56), channel_id=1, source_target_pairs={{128,0},{0,128},{129,1},{1,129},{130,2},{2,130},{131,3},{3,131},{1... | collective-permute-start | bytes 786440 | tf_op jit(solution)/shard_map/ppermute | solution.py:17

commit v10 on v9

--- a/solution.py
+++ b/solution.py
@@ -83,6 +83,13 @@
         out_ref[:, index] = flipped.astype(jnp.bfloat16)
 
 
+def tail_kernel(returned_ref, input_ref, filter_ref):
+    _, devices, group, rows = returned_ref.shape
+    for index, out_ref in enumerate([input_ref, filter_ref]):
+        block = returned_ref[index].astype(jnp.float32).reshape(devices * group, rows)
+        out_ref[...] = block.T.astype(out_ref.dtype)
+
+
 def body(grad_out, value_branch, key_gate, query_gate, short_weights, long_filters):
     rows, columns = grad_out.shape[1:]
     devices = lax.axis_size("seq")
@@ -118,9 +125,13 @@
     ).astype(jnp.bfloat16)
     outgoing = jnp.stack([grad_input, grad_filter.astype(jnp.bfloat16)])
     returned = lax.all_to_all(outgoing, "seq", split_axis=1, concat_axis=1, tiled=True)
-    input_tokens = returned[0].reshape(columns, rows).T
-    filter_back = returned[1].astype(jnp.float32)
-    filter_tokens = filter_back.reshape(columns, rows).T
+    input_tokens, filter_tokens = pl.pallas_call(
+        tail_kernel,
+        out_shape=(
+            jax.ShapeDtypeStruct((rows, columns), jnp.bfloat16),
+            jax.ShapeDtypeStruct((rows, columns), jnp.float32),
+        ),
+    )(returned)
     passed = shifted(input_tokens[None], "pipe", -1)
     return (passed, filter_tokens[None])
 

time: 81.6 us -> 84.2 us (1.032)
  Pallas kernels: 2.61 us -> 4.67 us
  waiting for transfers between devices: 22.6 us -> 23.8 us
    pallas_call x0 -> x1, Pallas kernels: none -> 2.06 us  [body(): pl.pallas_call(tail_kernel, out_shape=(jax.ShapeDtypeStruct((rows, column...]
    ppermute x1, waiting for transfers between devices: 0.11 us -> 1.37 us  [shifted(): return lax.ppermute(block, axis, route)]
    broadcast_in_dim x1 -> x0, local copies, waits for them, and re-layouts: 1 us -> none  [body(): return (passed, filter_tokens[None])]
    all_to_all x0 -> x1, local copies, waits for them, and re-layouts: none -> 0.84 us  [body(): lax.all_to_all(outgoing, 'seq', split_axis=1, concat_axis=1, tiled=True)]
  transfers between devices with their start and end apart: 2 -> 2, of which waited for: 2 -> 2; matrix products, arithmetic and copies ran while one was open for 4% -> 3% of each run, Pallas kernels for 0% -> 0%
where the time goes in v10:
time: 84.2 us; the launch traced here: 83.9 us
  waiting for transfers between devices  23.8 us (28%)
  blocking collectives  22.1 us (26%)
  starting transfers between devices  15.9 us (19%)
  matrix products  9.13 us (11%)
  Pallas kernels  4.67 us (6%)
  other arithmetic  4.24 us (5%)
  local copies, waits for them, and re-layouts  3.21 us (4%)
    all_to_all x1, waiting for transfers between devices, body(): recv = lax.all_to_all(send, 'seq', split_axis=0, concat_axis=0, tiled=True)  22.5 us
    all_to_all x1, blocking collectives, body(): lax.all_to_all(outgoing, 'seq', split_axis=1, concat_axis=1, tiled=True)  22.1 us
    all_to_all x1, starting transfers between devices, body(): recv = lax.all_to_all(send, 'seq', split_axis=0, concat_axis=0, tiled=True)  11.9 us
    dot_general x1, matrix products, forward(): spectrum = jnp.einsum('rd,shkr->shkd', table, twisted, precision=PRECISION)  4.13 us
    ppermute x1, starting transfers between devices, shifted(): return lax.ppermute(block, axis, route)  4.02 us
    dot_general x2, matrix products, contract(): jnp.einsum(form, jnp.asarray(table, jnp.float32), values, precision=PRECI...  3.09 us
    pallas_call x1, Pallas kernels, body(): pl.pallas_call(prep_kernel, out_shape=jax.ShapeDtypeStruct((devices, 4, g...  2.61 us
    pallas_call x1, Pallas kernels, body(): pl.pallas_call(tail_kernel, out_shape=(jax.ShapeDtypeStruct((rows, column...  2.06 us
  transfers between devices with their start and end apart: 2, of which 2 were waited for; matrix products, arithmetic and copies ran while one was open for 3% of the time, Pallas kernels for 0%

profile of v10, /device:TPU:1, one launch (start us, length us, event | category | flops | bytes accessed | tf_op | source)
XLA Modules:
  0.0 83.9 jit_solution(6267203329804223297)
XLA Ops:
  0.6 2.6 %shard_map.158 = bf16[32,4,16,256]{3,2,1,0:T(8,128)(2,1)} custom-call(bf16[256,512]{1,0:T(8,128)(2,1)} %bitcast.40, bf16[256,512]{1,0:T(8,128)(2,1)} %bitcast.41, bf16[256,512]{1,0:T(8,128)(2,1)} %bitcast.42, bf16[256,512]{1,0:T(8,128)(2,1)} %bitcast.43, bf16[256,512]{1,0:T(8,128)(2,1)} %bitcast.44), custom_call_target="tpu_custom_call" | custom-call | tf_op jit(solution)/shard_map/pallas_call | solution.py:99
  3.2 11.9 %all-to-all-start = ((bf16[32,4,16,256]{3,2,1,0:T(8,128)(2,1)}), bf16[32,4,16,256]{3,2,1,0:T(8,128)(2,1)S(1)}, u32[]{:S(2)}, u32[]{:S(2)}) async-start(bf16[32,4,16,256]{3,2,1,0:T(8,128)(2,1)} %shard_map.158), calls=%async_computation | async-start | bytes 2097152 | tf_op jit(solution)/shard_map/all_to_all | solution.py:102
  15.1 0.8 fusion.54
  16.2 0.2 fusion.31
  16.4 1.1 %fusion.23 = (f32[256,256]{1,0:T(8,128)S(1)}, f32[256,256]{1,0:T(8,128)S(1)}, f32[256,256]{1,0:T(8,128)S(1)}) fusion(s32[256]{0:T(256)S(1)} %iota.6), kind=kLoop, calls=%fused_computation.48 | loop fusion | flops 983040 | bytes 787456 | tf_op jit(solution)/shard_map/neg | solution.py:36
  17.5 22.5 %all-to-all-done = bf16[32,4,16,256]{3,2,1,0:T(8,128)(2,1)S(1)} async-done(((bf16[32,4,16,256]{3,2,1,0:T(8,128)(2,1)}), bf16[32,4,16,256]{3,2,1,0:T(8,128)(2,1)S(1)}, u32[]{:S(2)}, u32[]{:S(2)}) %all-to-all-start) | async-done | bytes 1048608 | tf_op jit(solution)/shard_map/all_to_all | solution.py:102
  40.0 1.2 %convolution_bitcast_fusion = f32[3,66,16,256]{3,1,2,0:T(8,128)S(1)} fusion(bf16[32,3,16,256]{3,2,1,0:T(8,128)(2,1)S(1)} %slice.93, f32[33,32]{0,1:T(8,128)S(1)} %get-tuple-element.25, f32[33,32]{0,1:T(8,128)S(1)} %get-tuple-element.24), kind=kOutput, calls=%fused_computation.14 | convolution fusion | flops 155715648 | bytes 4038912 | tf_op jit(solution)/shard_map/ja,sakr->sjkr/dot_general | solution.py:28
  41.2 0.5 multiply_add_fusion
  41.8 0.6 pad_maximum_fusion
  42.4 4.1 %fusion = f32[3,33,16,512]{3,2,1,0:T(8,128)S(1)} fusion(f32[3,33,16,512]{3,1,2,0:T(8,128)S(1)} %pad_maximum_fusion, f32[256,256]{1,0:T(8,128)S(1)} %get-tuple-element.19, f32[256,256]{1,0:T(8,128)S(1)} %get-tuple-element.18, f32[256,256]{1,0:T(8,128)S(1)} %get-tuple-element.17), kind=kOutput, calls=%fused_computation.1 | convolution fusion | flops 2492203008 | bytes 7274496 | tf_op jit(solution)/shard_map/rd,shkr->shkd/dot_general | solution.py:50
  46.5 0.3 multiply_add_fusion.3
  46.9 1.9 %fusion.4 = f32[2,33,16,512]{3,2,1,0:T(8,128)S(1)} fusion(f32[1,33,16,256]{3,2,1,0:T(8,128)S(1)} %get-tuple-element.11, f32[1,33,16,256]{3,2,1,0:T(8,128)S(1)} %get-tuple-element.10, f32[1,33,16,256]{3,2,1,0:T(8,128)S(1)} %get-tuple-element.9, f32[1,33,16,256]{3,2,1,0:T(8,128)S(1)} %get-tuple-element.8, f32[256,256]{1,0:T(8,128)S(1)} %get-tuple-element.19, ...), kind=kOutput, calls=%fused_computation.5 | convolution fusion | flops 1663352832 | bytes 5111808 | tf_op jit(solution)/shard_map/rd,shkd->shkr/dot_general | solution.py:58
  48.8 0.4 multiply_subtract_fusion.1
  49.2 0.2 pad_maximum_fusion.1
  49.3 0.5 copy-done
  49.8 1.9 %fusion.2 = f32[32,2,16,256]{3,0,2,1:T(8,128)S(1)} fusion(f32[2,66,16,256]{3,2,1,0:T(8,128)S(1)} %pad_maximum_fusion.1, f32[32,33]{1,0:T(8,128)S(1)} %get-tuple-element.21, f32[32,33]{1,0:T(8,128)S(1)} %get-tuple-element.20, f32[66]{0:T(128)S(1)} %copy-done), kind=kOutput, calls=%fused_computation.3 | convolution fusion | flops 103813248 | bytes 3219976 | tf_op jit(solution)/shard_map/ac,sckr->askr/dot_general | solution.py:28
  52.0 0.4 fusion.19
  52.5 0.3 copy.27
  52.8 22.1 %all_to_all.10 = bf16[2,32,16,256]{3,2,0,1:T(8,128)(2,1)S(1)} all-to-all(bf16[2,32,16,256]{3,2,0,1:T(8,128)(2,1)S(1)} %copy.27), channel_id=1, replica_groups=mesh['pipe'=2,'seq'=32,'chan'=4] {'seq'}, dimensions={1} | all-to-all | bytes 1048576 | tf_op jit(solution)/shard_map/all_to_all | solution.py:127
  74.9 0.8 %copy.28.returned_ref = bf16[2,32,16,256]{3,2,1,0:T(8,128)(2,1)} copy(bf16[2,32,16,256]{3,2,0,1:T(8,128)(2,1)S(1)} %all_to_all.10) | data formatting | bytes 1048576 | tf_op jit(solution)/shard_map/all_to_all | solution.py:127
  75.7 2.1 %shard_map.159 = (bf16[256,512]{1,0:T(8,128)(2,1)}, f32[256,512]{1,0:T(8,128)}) custom-call(bf16[2,32,16,256]{3,2,1,0:T(8,128)(2,1)} %copy.28.returned_ref), custom_call_target="tpu_custom_call" | custom-call | tf_op jit(solution)/shard_map/pallas_call | solution.py:128
  77.8 4.0 %collective-permute-start = (bf16[1,256,512]{2,1,0:T(8,128)(2,1)}, bf16[1,256,512]{2,1,0:T(8,128)(2,1)S(1)}, u32[]{:S(2)}, u32[]{:S(2)}) collective-permute-start(bf16[1,256,512]{2,1,0:T(8,128)(2,1)} %bitcast.46), channel_id=1, source_target_pairs={{128,0},{0,128},{129,1},{1,129},{130,2},{2,130},{131,3},{3,131},{1... | collective-permute-start | bytes 786440 | tf_op jit(solution)/shard_map/ppermute | solution.py:17
  81.8 1.4 %collective-permute-done = bf16[1,256,512]{2,1,0:T(8,128)(2,1)S(1)} collective-permute-done((bf16[1,256,512]{2,1,0:T(8,128)(2,1)}, bf16[1,256,512]{2,1,0:T(8,128)(2,1)S(1)}, u32[]{:S(2)}, u32[]{:S(2)}) %collective-permute-start) | collective-permute-done | bytes 262176 | tf_op jit(solution)/shard_map/ppermute | solution.py:17
  83.2 0.7 copy.42
  (13 shorter events, 0.6 us)
Async XLA Ops:
  3.2 36.7 %all-to-all-start = ((bf16[32,4,16,256]{3,2,1,0:T(8,128)(2,1)}), bf16[32,4,16,256]{3,2,1,0:T(8,128)(2,1)S(1)}, u32[]{:S(2)}, u32[]{:S(2)}) async-start(bf16[32,4,16,256]{3,2,1,0:T(8,128)(2,1)} %shard_map.158), calls=%async_computation | async-start | bytes 2097152 | tf_op jit(solution)/shard_map/all_to_all | solution.py:102
  49.1 0.7 copy-start
  77.8 5.4 %collective-permute-start = (bf16[1,256,512]{2,1,0:T(8,128)(2,1)}, bf16[1,256,512]{2,1,0:T(8,128)(2,1)S(1)}, u32[]{:S(2)}, u32[]{:S(2)}) collective-permute-start(bf16[1,256,512]{2,1,0:T(8,128)(2,1)} %bitcast.46), channel_id=1, source_target_pairs={{128,0},{0,128},{129,1},{1,129},{130,2},{2,130},{131,3},{3,131},{1... | collective-permute-start | bytes 786440 | tf_op jit(solution)/shard_map/ppermute | solution.py:17

commit v11 on v9

--- a/solution.py
+++ b/solution.py
@@ -79,8 +79,7 @@
     gated_value = (key * value_ref[...].astype(jnp.float32)).astype(jnp.bfloat16)
     devices, _, group, rows = out_ref.shape
     for index, block in enumerate([grad_conv, gated_value, filter_ref[...], key_ref[...]]):
-        flipped = block.astype(jnp.float32).T.reshape(devices, group, rows)
-        out_ref[:, index] = flipped.astype(jnp.bfloat16)
+        out_ref[:, index] = block.T.reshape(devices, group, rows)
 
 
 def body(grad_out, value_branch, key_gate, query_gate, short_weights, long_filters):

time: 81.6 us -> 81.5 us (level)
  no operation moved by 1% of the time
where the time goes in v11:
time: 81.5 us; the launch traced here: 81.2 us
  waiting for transfers between devices  22.6 us (28%)
  blocking collectives  22.1 us (27%)
  starting transfers between devices  16 us (20%)
  matrix products  9.31 us (11%)
  other arithmetic  4.42 us (5%)
  local copies, waits for them, and re-layouts  3.46 us (4%)
  Pallas kernels  2.57 us (3%)
  between operations  0.85 us (1%)
    all_to_all x1, waiting for transfers between devices, body(): recv = lax.all_to_all(send, 'seq', split_axis=0, concat_axis=0, tiled=True)  22.4 us
    all_to_all x1, blocking collectives, body(): lax.all_to_all(outgoing, 'seq', split_axis=1, concat_axis=1, tiled=True)  22.1 us
    all_to_all x1, starting transfers between devices, body(): recv = lax.all_to_all(send, 'seq', split_axis=0, concat_axis=0, tiled=True)  11.9 us
    dot_general x1, matrix products, forward(): spectrum = jnp.einsum('rd,shkr->shkd', table, twisted, precision=PRECISION)  4.13 us
    ppermute x1, starting transfers between devices, shifted(): return lax.ppermute(block, axis, route)  4.1 us
    dot_general x2, matrix products, contract(): jnp.einsum(form, jnp.asarray(table, jnp.float32), values, precision=PRECI...  3.26 us
    pallas_call x1, Pallas kernels, body(): pl.pallas_call(prep_kernel, out_shape=jax.ShapeDtypeStruct((devices, 4, g...  2.57 us
    dot_general x1, matrix products, inverse(): jnp.einsum('rd,shkd->shkr', table, jnp.concatenate([real, imag], axis=-1)...  1.91 us
  transfers between devices with their start and end apart: 2, of which 2 were waited for; matrix products, arithmetic and copies ran while one was open for 4% of the time, Pallas kernels for 0%

profile of v11, /device:TPU:1, one launch (start us, length us, event | category | flops | bytes accessed | tf_op | source)
XLA Modules:
  0.0 81.2 jit_solution(32875296847674220)
XLA Ops:
  0.6 2.6 %shard_map.158 = bf16[32,4,16,256]{3,2,1,0:T(8,128)(2,1)} custom-call(bf16[256,512]{1,0:T(8,128)(2,1)} %bitcast.51, bf16[256,512]{1,0:T(8,128)(2,1)} %bitcast.52, bf16[256,512]{1,0:T(8,128)(2,1)} %bitcast.53, bf16[256,512]{1,0:T(8,128)(2,1)} %bitcast.54, bf16[256,512]{1,0:T(8,128)(2,1)} %bitcast.55), custom_call_target="tpu_custom_call" | custom-call | tf_op jit(solution)/shard_map/pallas_call | solution.py:91
  3.2 11.9 %all-to-all-start = ((bf16[32,4,16,256]{3,2,1,0:T(8,128)(2,1)}), bf16[32,4,16,256]{3,2,1,0:T(8,128)(2,1)S(1)}, u32[]{:S(2)}, u32[]{:S(2)}) async-start(bf16[32,4,16,256]{3,2,1,0:T(8,128)(2,1)} %shard_map.158), calls=%async_computation | async-start | bytes 2097152 | tf_op jit(solution)/shard_map/all_to_all | solution.py:94
  15.1 0.8 fusion.55
  16.0 0.2 fusion.53
  16.1 0.2 fusion.32
  16.4 1.1 %fusion.24 = (f32[256,256]{1,0:T(8,128)S(1)}, f32[256,256]{1,0:T(8,128)S(1)}, f32[256,256]{1,0:T(8,128)S(1)}) fusion(s32[256]{0:T(256)S(1)} %iota.6), kind=kLoop, calls=%fused_computation.50 | loop fusion | flops 983040 | bytes 787456 | tf_op jit(solution)/shard_map/neg | solution.py:36
  17.5 22.4 %all-to-all-done = bf16[32,4,16,256]{3,2,1,0:T(8,128)(2,1)S(1)} async-done(((bf16[32,4,16,256]{3,2,1,0:T(8,128)(2,1)}), bf16[32,4,16,256]{3,2,1,0:T(8,128)(2,1)S(1)}, u32[]{:S(2)}, u32[]{:S(2)}) %all-to-all-start) | async-done | bytes 1048608 | tf_op jit(solution)/shard_map/all_to_all | solution.py:94
  40.0 1.2 %convolution_bitcast_fusion = f32[3,66,16,256]{3,1,2,0:T(8,128)S(1)} fusion(bf16[3,32,16,256]{3,2,0,1:T(8,128)(2,1)S(1)} %slice_bitcast_fusion, f32[33,32]{0,1:T(8,128)S(1)} %get-tuple-element.23, f32[33,32]{0,1:T(8,128)S(1)} %get-tuple-element.22), kind=kOutput, calls=%fused_computation.14 | convolution fusion | flops 155715648 | bytes 4038912 | tf_op jit(solution)/shard_map/ja,sakr->sjkr/dot_general | solution.py:28
  41.2 0.5 multiply_add_fusion
  41.8 0.6 pad_maximum_fusion
  42.4 4.1 %fusion = f32[3,33,16,512]{3,2,1,0:T(8,128)S(1)} fusion(f32[3,33,16,512]{3,1,2,0:T(8,128)S(1)} %pad_maximum_fusion, f32[256,256]{1,0:T(8,128)S(1)} %get-tuple-element.17, f32[256,256]{1,0:T(8,128)S(1)} %get-tuple-element.16, f32[256,256]{1,0:T(8,128)S(1)} %get-tuple-element.15), kind=kOutput, calls=%fused_computation.1 | convolution fusion | flops 2492203008 | bytes 7274496 | tf_op jit(solution)/shard_map/rd,shkr->shkd/dot_general | solution.py:50
  46.5 0.3 multiply_add_fusion.3
  46.8 1.9 %fusion.4 = f32[2,33,16,512]{3,2,1,0:T(8,128)S(1)} fusion(f32[1,33,16,256]{3,2,1,0:T(8,128)S(1)} %get-tuple-element.7, f32[1,33,16,256]{3,2,1,0:T(8,128)S(1)} %get-tuple-element.6, f32[1,33,16,256]{3,2,1,0:T(8,128)S(1)} %get-tuple-element.5, f32[1,33,16,256]{3,2,1,0:T(8,128)S(1)} %get-tuple-element.4, f32[256,256]{1,0:T(8,128)S(1)} %get-tuple-element.17, ...), kind=kOutput, calls=%fused_computation.5 | convolution fusion | flops 1663352832 | bytes 5111808 | tf_op jit(solution)/shard_map/rd,shkd->shkr/dot_general | solution.py:58
  48.7 0.4 multiply_subtract_fusion.1
  49.1 0.2 pad_maximum_fusion.1
  49.3 0.5 copy-done
  49.8 2.1 %fusion.2 = f32[32,2,16,256]{3,0,2,1:T(8,128)S(1)} fusion(f32[2,66,16,256]{3,2,1,0:T(8,128)S(1)} %pad_maximum_fusion.1, f32[32,33]{1,0:T(8,128)S(1)} %get-tuple-element.19, f32[32,33]{1,0:T(8,128)S(1)} %get-tuple-element.18, f32[66]{0:T(128)S(1)} %copy-done), kind=kOutput, calls=%fused_computation.3 | convolution fusion | flops 103813248 | bytes 3219976 | tf_op jit(solution)/shard_map/ac,sckr->askr/dot_general | solution.py:28
  51.9 0.3 fusion.16
  52.3 0.2 copy.49
  52.5 0.4 fusion.20
  53.0 22.1 %all_to_all.10 = bf16[2,32,16,256]{3,2,0,1:T(8,128)(2,1)S(1)} all-to-all(bf16[2,32,16,256]{3,2,0,1:T(8,128)(2,1)S(1)} %copy.29), channel_id=1, replica_groups=mesh['pipe'=2,'seq'=32,'chan'=4] {'seq'}, dimensions={1} | all-to-all | bytes 1048576 | tf_op jit(solution)/shard_map/all_to_all | solution.py:119
  75.3 4.1 %collective-permute-start = (bf16[1,256,512]{2,1,0:T(8,128)(2,1)S(1)}, bf16[1,256,512]{2,1,0:T(8,128)(2,1)S(1)}, u32[]{:S(2)}, u32[]{:S(2)}) collective-permute-start(bf16[1,256,512]{2,1,0:T(8,128)(2,1)S(1)} %bitcast.56), channel_id=1, source_target_pairs={{128,0},{0,128},{129,1},{1,129},{130,2},{2,130},{131,3},{3,131},{1... | collective-permute-start | bytes 786440 | tf_op jit(solution)/shard_map/ppermute | solution.py:17
  79.4 1.0 %copy.31 = f32[512,256]{0,1:T(8,128)} copy(f32[512,256]{1,0:T(8,128)S(1)} %bitcast_convert_fusion) | data formatting | bytes 1048576 | tf_op jit(solution)/shard_map/broadcast_in_dim | solution.py:124
  80.5 0.7 copy.51
  (16 shorter events, 0.7 us)
Async XLA Ops:
  3.2 36.7 %all-to-all-start = ((bf16[32,4,16,256]{3,2,1,0:T(8,128)(2,1)}), bf16[32,4,16,256]{3,2,1,0:T(8,128)(2,1)S(1)}, u32[]{:S(2)}, u32[]{:S(2)}) async-start(bf16[32,4,16,256]{3,2,1,0:T(8,128)(2,1)} %shard_map.158), calls=%async_computation | async-start | bytes 2097152 | tf_op jit(solution)/shard_map/all_to_all | solution.py:94
  49.1 0.7 copy-start
  75.3 5.3 %collective-permute-start = (bf16[1,256,512]{2,1,0:T(8,128)(2,1)S(1)}, bf16[1,256,512]{2,1,0:T(8,128)(2,1)S(1)}, u32[]{:S(2)}, u32[]{:S(2)}) collective-permute-start(bf16[1,256,512]{2,1,0:T(8,128)(2,1)S(1)} %bitcast.56), channel_id=1, source_target_pairs={{128,0},{0,128},{129,1},{1,129},{130,2},{2,130},{131,3},{3,131},{1... | collective-permute-start | bytes 786440 | tf_op jit(solution)/shard_map/ppermute | solution.py:17

commit v12 on v11

--- a/solution.py
+++ b/solution.py
@@ -46,7 +46,9 @@
     cos_t, sin_t = angle_table(half, np.arange(rows), padded)
     cos_t = cos_t[:, None, :]
     sin_t = sin_t[:, None, :]
-    twisted = jnp.concatenate([real * cos_t + imag * sin_t, imag * cos_t - real * sin_t], axis=-1)
+    twisted = jnp.concatenate([real, imag], axis=-1) * jnp.concatenate([cos_t, cos_t], axis=-1) + jnp.concatenate(
+        [imag, real], axis=-1
+    ) * jnp.concatenate([sin_t, -sin_t], axis=-1)
     spectrum = jnp.einsum("rd,shkr->shkd", table, twisted, precision=PRECISION)
     return spectrum[..., :rows], spectrum[..., rows:]
 

time: 81.5 us -> 81.5 us (level)
  transfers between devices with their start and end apart: 2 -> 2, of which waited for: 2 -> 2; matrix products, arithmetic and copies ran while one was open for 4% -> 5% of each run, Pallas kernels for 0% -> 0%
where the time goes in v12:
time: 81.5 us; the launch traced here: 81.2 us
  waiting for transfers between devices  22.3 us (27%)
  blocking collectives  22.1 us (27%)
  starting transfers between devices  16 us (20%)
  matrix products  9.32 us (11%)
  other arithmetic  4.28 us (5%)
  local copies, waits for them, and re-layouts  3.83 us (5%)
  Pallas kernels  2.58 us (3%)
  between operations  0.87 us (1%)
    all_to_all x1, waiting for transfers between devices, body(): recv = lax.all_to_all(send, 'seq', split_axis=0, concat_axis=0, tiled=True)  22.2 us
    all_to_all x1, blocking collectives, body(): lax.all_to_all(outgoing, 'seq', split_axis=1, concat_axis=1, tiled=True)  22.1 us
    all_to_all x1, starting transfers between devices, body(): recv = lax.all_to_all(send, 'seq', split_axis=0, concat_axis=0, tiled=True)  11.9 us
    dot_general x1, matrix products, forward(): spectrum = jnp.einsum('rd,shkr->shkd', table, twisted, precision=PRECISION)  4.12 us
    ppermute x1, starting transfers between devices, shifted(): return lax.ppermute(block, axis, route)  4.1 us
    dot_general x2, matrix products, contract(): jnp.einsum(form, jnp.asarray(table, jnp.float32), values, precision=PRECI...  3.28 us
    pallas_call x1, Pallas kernels, body(): pl.pallas_call(prep_kernel, out_shape=jax.ShapeDtypeStruct((devices, 4, g...  2.58 us
    dot_general x1, matrix products, inverse(): jnp.einsum('rd,shkd->shkr', table, jnp.concatenate([real, imag], axis=-1)...  1.91 us
  transfers between devices with their start and end apart: 2, of which 2 were waited for; matrix products, arithmetic and copies ran while one was open for 5% of the time, Pallas kernels for 0%

profile of v12, /device:TPU:1, one launch (start us, length us, event | category | flops | bytes accessed | tf_op | source)
XLA Modules:
  0.0 81.2 jit_solution(9713252329416780762)
XLA Ops:
  0.6 2.6 %shard_map.158 = bf16[32,4,16,256]{3,2,1,0:T(8,128)(2,1)} custom-call(bf16[256,512]{1,0:T(8,128)(2,1)} %bitcast.55, bf16[256,512]{1,0:T(8,128)(2,1)} %bitcast.56, bf16[256,512]{1,0:T(8,128)(2,1)} %bitcast.57, bf16[256,512]{1,0:T(8,128)(2,1)} %bitcast.58, bf16[256,512]{1,0:T(8,128)(2,1)} %bitcast.59), custom_call_target="tpu_custom_call" | custom-call | tf_op jit(solution)/shard_map/pallas_call | solution.py:93
  3.2 11.9 %all-to-all-start = ((bf16[32,4,16,256]{3,2,1,0:T(8,128)(2,1)}), bf16[32,4,16,256]{3,2,1,0:T(8,128)(2,1)S(1)}, u32[]{:S(2)}, u32[]{:S(2)}) async-start(bf16[32,4,16,256]{3,2,1,0:T(8,128)(2,1)} %shard_map.158), calls=%async_computation | async-start | bytes 2097152 | tf_op jit(solution)/shard_map/all_to_all | solution.py:96
  15.1 0.8 fusion.65
  15.9 0.2 fusion.41
  16.2 0.2 fusion.63
  16.4 0.2 fusion.39
  16.6 1.1 %fusion.25 = (f32[256,256]{1,0:T(8,128)S(1)}, f32[256,256]{1,0:T(8,128)S(1)}, f32[256,256]{1,0:T(8,128)S(1)}) fusion(s32[256]{0:T(256)S(1)} %iota.6), kind=kLoop, calls=%fused_computation.50 | loop fusion | flops 983040 | bytes 787456 | tf_op jit(solution)/shard_map/neg | solution.py:36
  17.8 22.2 %all-to-all-done = bf16[32,4,16,256]{3,2,1,0:T(8,128)(2,1)S(1)} async-done(((bf16[32,4,16,256]{3,2,1,0:T(8,128)(2,1)}), bf16[32,4,16,256]{3,2,1,0:T(8,128)(2,1)S(1)}, u32[]{:S(2)}, u32[]{:S(2)}) %all-to-all-start) | async-done | bytes 1048608 | tf_op jit(solution)/shard_map/all_to_all | solution.py:96
  40.0 1.2 %convolution_bitcast_fusion = f32[3,66,16,256]{3,1,2,0:T(8,128)S(1)} fusion(bf16[3,32,16,256]{3,2,0,1:T(8,128)(2,1)S(1)} %slice_bitcast_fusion, f32[33,32]{0,1:T(8,128)S(1)} %get-tuple-element.26, f32[33,32]{0,1:T(8,128)S(1)} %get-tuple-element.25), kind=kOutput, calls=%fused_computation.16 | convolution fusion | flops 155715648 | bytes 4038912 | tf_op jit(solution)/shard_map/ja,sakr->sjkr/dot_general | solution.py:28
  41.2 0.4 fusion.71
  41.6 0.7 fusion
  42.3 4.1 %fusion.1 = f32[3,33,16,512]{3,2,1,0:T(8,128)S(1)} fusion(f32[3,33,16,512]{3,1,2,0:T(8,128)S(1)} %fusion, f32[256,256]{1,0:T(8,128)S(1)} %get-tuple-element.17, f32[256,256]{1,0:T(8,128)S(1)} %get-tuple-element.16, f32[256,256]{1,0:T(8,128)S(1)} %get-tuple-element.15), kind=kOutput, calls=%fused_computation.3 | convolution fusion | flops 2492203008 | bytes 7274496 | tf_op jit(solution)/shard_map/rd,shkr->shkd/dot_general | solution.py:52
  46.5 0.3 multiply_add_fusion.2
  46.8 1.9 %fusion.5 = f32[2,33,16,512]{3,2,1,0:T(8,128)S(1)} fusion(f32[1,33,16,256]{3,2,1,0:T(8,128)S(1)} %get-tuple-element.7, f32[1,33,16,256]{3,2,1,0:T(8,128)S(1)} %get-tuple-element.6, f32[1,33,16,256]{3,2,1,0:T(8,128)S(1)} %get-tuple-element.5, f32[1,33,16,256]{3,2,1,0:T(8,128)S(1)} %get-tuple-element.4, f32[256,256]{1,0:T(8,128)S(1)} %get-tuple-element.17, ...), kind=kOutput, calls=%fused_computation.7 | convolution fusion | flops 1663352832 | bytes 5111808 | tf_op jit(solution)/shard_map/rd,shkd->shkr/dot_general | solution.py:60
  48.7 0.4 multiply_subtract_fusion
  49.1 0.2 pad_maximum_fusion
  49.3 0.5 copy-done
  49.7 2.1 %fusion.3 = f32[32,2,16,256]{3,0,2,1:T(8,128)S(1)} fusion(f32[2,66,16,256]{3,2,1,0:T(8,128)S(1)} %pad_maximum_fusion, f32[32,33]{1,0:T(8,128)S(1)} %get-tuple-element.19, f32[32,33]{1,0:T(8,128)S(1)} %get-tuple-element.18, f32[66]{0:T(128)S(1)} %copy-done), kind=kOutput, calls=%fused_computation.5 | convolution fusion | flops 103813248 | bytes 3219976 | tf_op jit(solution)/shard_map/ac,sckr->askr/dot_general | solution.py:28
  51.9 0.3 fusion.17
  52.5 0.4 fusion.21
  53.0 22.1 %all_to_all.10 = bf16[2,32,16,256]{3,2,0,1:T(8,128)(2,1)S(1)} all-to-all(bf16[2,32,16,256]{3,2,0,1:T(8,128)(2,1)S(1)} %copy.29), channel_id=1, replica_groups=mesh['pipe'=2,'seq'=32,'chan'=4] {'seq'}, dimensions={1} | all-to-all | bytes 1048576 | tf_op jit(solution)/shard_map/all_to_all | solution.py:121
  75.3 4.1 %collective-permute-start = (bf16[1,256,512]{2,1,0:T(8,128)(2,1)S(1)}, bf16[1,256,512]{2,1,0:T(8,128)(2,1)S(1)}, u32[]{:S(2)}, u32[]{:S(2)}) collective-permute-start(bf16[1,256,512]{2,1,0:T(8,128)(2,1)S(1)} %bitcast.60), channel_id=1, source_target_pairs={{128,0},{0,128},{129,1},{1,129},{130,2},{2,130},{131,3},{3,131},{1... | collective-permute-start | bytes 786440 | tf_op jit(solution)/shard_map/ppermute | solution.py:17
  79.4 1.0 %copy.31 = f32[512,256]{0,1:T(8,128)} copy(f32[512,256]{1,0:T(8,128)S(1)} %bitcast_convert_fusion) | data formatting | bytes 1048576 | tf_op jit(solution)/shard_map/broadcast_in_dim | solution.py:126
  80.5 0.7 copy.51
  (18 shorter events, 0.9 us)
Async XLA Ops:
  3.2 36.7 %all-to-all-start = ((bf16[32,4,16,256]{3,2,1,0:T(8,128)(2,1)}), bf16[32,4,16,256]{3,2,1,0:T(8,128)(2,1)S(1)}, u32[]{:S(2)}, u32[]{:S(2)}) async-start(bf16[32,4,16,256]{3,2,1,0:T(8,128)(2,1)} %shard_map.158), calls=%async_computation | async-start | bytes 2097152 | tf_op jit(solution)/shard_map/all_to_all | solution.py:96
  49.1 0.7 copy-start
  75.3 5.3 %collective-permute-start = (bf16[1,256,512]{2,1,0:T(8,128)(2,1)S(1)}, bf16[1,256,512]{2,1,0:T(8,128)(2,1)S(1)}, u32[]{:S(2)}, u32[]{:S(2)}) collective-permute-start(bf16[1,256,512]{2,1,0:T(8,128)(2,1)S(1)} %bitcast.60), channel_id=1, source_target_pairs={{128,0},{0,128},{129,1},{1,129},{130,2},{2,130},{131,3},{3,131},{1... | collective-permute-start | bytes 786440 | tf_op jit(solution)/shard_map/ppermute | solution.py:17

commit v13 on v11

--- a/solution.py
+++ b/solution.py
@@ -88,8 +88,14 @@
     position = lax.axis_index("seq")
     group = columns // devices
     padded = 2 * rows * devices
+    steps = 4 if devices % 4 == 0 else 1
+    width = columns // steps
     send = pl.pallas_call(
-        prep_kernel, out_shape=jax.ShapeDtypeStruct((devices, 4, group, rows), jnp.bfloat16)
+        prep_kernel,
+        grid=(steps,),
+        in_specs=[pl.BlockSpec((rows, width), lambda i: (0, i))] * 5,
+        out_specs=pl.BlockSpec((devices // steps, 4, group, rows), lambda i: (i, 0, 0, 0)),
+        out_shape=jax.ShapeDtypeStruct((devices, 4, group, rows), jnp.bfloat16),
     )(grad_out[0], value_branch[0], key_gate[0], query_gate[0], long_filters[0])
     recv = lax.all_to_all(send, "seq", split_axis=0, concat_axis=0, tiled=True)
     table = row_table(rows)

time: 81.5 us -> 82.8 us (1.016)
  Pallas kernels: 2.57 us -> 3.66 us
    pallas_call x1, Pallas kernels: 2.57 us -> 3.66 us  [body(): pl.pallas_call(prep_kernel, grid=(steps,), in_specs=[pl.BlockSpec((rows,...]
where the time goes in v13:
time: 82.8 us; the launch traced here: 82.3 us
  waiting for transfers between devices  22.6 us (27%)
  blocking collectives  22.1 us (27%)
  starting transfers between devices  16 us (19%)
  matrix products  9.31 us (11%)
  other arithmetic  4.42 us (5%)
  Pallas kernels  3.66 us (4%)
  local copies, waits for them, and re-layouts  3.46 us (4%)
  between operations  0.85 us (1%)
    all_to_all x1, waiting for transfers between devices, body(): recv = lax.all_to_all(send, 'seq', split_axis=0, concat_axis=0, tiled=True)  22.4 us
    all_to_all x1, blocking collectives, body(): lax.all_to_all(outgoing, 'seq', split_axis=1, concat_axis=1, tiled=True)  22.1 us
    all_to_all x1, starting transfers between devices, body(): recv = lax.all_to_all(send, 'seq', split_axis=0, concat_axis=0, tiled=True)  11.9 us
    dot_general x1, matrix products, forward(): spectrum = jnp.einsum('rd,shkr->shkd', table, twisted, precision=PRECISION)  4.13 us
    ppermute x1, starting transfers between devices, shifted(): return lax.ppermute(block, axis, route)  4.11 us
    pallas_call x1, Pallas kernels, body(): pl.pallas_call(prep_kernel, grid=(steps,), in_specs=[pl.BlockSpec((rows,...  3.66 us
    dot_general x2, matrix products, contract(): jnp.einsum(form, jnp.asarray(table, jnp.float32), values, precision=PRECI...  3.26 us
    dot_general x1, matrix products, inverse(): jnp.einsum('rd,shkd->shkr', table, jnp.concatenate([real, imag], axis=-1)...  1.91 us
  transfers between devices with their start and end apart: 2, of which 2 were waited for; matrix products, arithmetic and copies ran while one was open for 4% of the time, Pallas kernels for 0%

profile of v13, /device:TPU:1, one launch (start us, length us, event | category | flops | bytes accessed | tf_op | source)
XLA Modules:
  0.0 82.3 jit_solution(8103314018395096144)
XLA Ops:
  0.6 3.7 %shard_map.158 = bf16[32,4,16,256]{3,2,1,0:T(8,128)(2,1)} custom-call(bf16[256,512]{1,0:T(8,128)(2,1)} %bitcast.51, bf16[256,512]{1,0:T(8,128)(2,1)} %bitcast.52, bf16[256,512]{1,0:T(8,128)(2,1)} %bitcast.53, bf16[256,512]{1,0:T(8,128)(2,1)} %bitcast.54, bf16[256,512]{1,0:T(8,128)(2,1)} %bitcast.55), custom_call_target="tpu_custom_call" | custom-call | tf_op jit(solution)/shard_map/pallas_call | solution.py:93
  4.3 11.9 %all-to-all-start = ((bf16[32,4,16,256]{3,2,1,0:T(8,128)(2,1)}), bf16[32,4,16,256]{3,2,1,0:T(8,128)(2,1)S(1)}, u32[]{:S(2)}, u32[]{:S(2)}) async-start(bf16[32,4,16,256]{3,2,1,0:T(8,128)(2,1)} %shard_map.158), calls=%async_computation | async-start | bytes 2097152 | tf_op jit(solution)/shard_map/all_to_all | solution.py:100
  16.2 0.8 fusion.55
  17.0 0.2 fusion.53
  17.2 0.2 fusion.32
  17.5 1.1 %fusion.24 = (f32[256,256]{1,0:T(8,128)S(1)}, f32[256,256]{1,0:T(8,128)S(1)}, f32[256,256]{1,0:T(8,128)S(1)}) fusion(s32[256]{0:T(256)S(1)} %iota.6), kind=kLoop, calls=%fused_computation.50 | loop fusion | flops 983040 | bytes 787456 | tf_op jit(solution)/shard_map/neg | solution.py:36
  18.6 22.4 %all-to-all-done = bf16[32,4,16,256]{3,2,1,0:T(8,128)(2,1)S(1)} async-done(((bf16[32,4,16,256]{3,2,1,0:T(8,128)(2,1)}), bf16[32,4,16,256]{3,2,1,0:T(8,128)(2,1)S(1)}, u32[]{:S(2)}, u32[]{:S(2)}) %all-to-all-start) | async-done | bytes 1048608 | tf_op jit(solution)/shard_map/all_to_all | solution.py:100
  41.1 1.2 %convolution_bitcast_fusion = f32[3,66,16,256]{3,1,2,0:T(8,128)S(1)} fusion(bf16[3,32,16,256]{3,2,0,1:T(8,128)(2,1)S(1)} %slice_bitcast_fusion, f32[33,32]{0,1:T(8,128)S(1)} %get-tuple-element.23, f32[33,32]{0,1:T(8,128)S(1)} %get-tuple-element.22), kind=kOutput, calls=%fused_computation.14 | convolution fusion | flops 155715648 | bytes 4038912 | tf_op jit(solution)/shard_map/ja,sakr->sjkr/dot_general | solution.py:28
  42.3 0.5 multiply_add_fusion
  42.8 0.6 pad_maximum_fusion
  43.5 4.1 %fusion = f32[3,33,16,512]{3,2,1,0:T(8,128)S(1)} fusion(f32[3,33,16,512]{3,1,2,0:T(8,128)S(1)} %pad_maximum_fusion, f32[256,256]{1,0:T(8,128)S(1)} %get-tuple-element.17, f32[256,256]{1,0:T(8,128)S(1)} %get-tuple-element.16, f32[256,256]{1,0:T(8,128)S(1)} %get-tuple-element.15), kind=kOutput, calls=%fused_computation.1 | convolution fusion | flops 2492203008 | bytes 7274496 | tf_op jit(solution)/shard_map/rd,shkr->shkd/dot_general | solution.py:50
  47.6 0.3 multiply_add_fusion.3
  47.9 1.9 %fusion.4 = f32[2,33,16,512]{3,2,1,0:T(8,128)S(1)} fusion(f32[1,33,16,256]{3,2,1,0:T(8,128)S(1)} %get-tuple-element.7, f32[1,33,16,256]{3,2,1,0:T(8,128)S(1)} %get-tuple-element.6, f32[1,33,16,256]{3,2,1,0:T(8,128)S(1)} %get-tuple-element.5, f32[1,33,16,256]{3,2,1,0:T(8,128)S(1)} %get-tuple-element.4, f32[256,256]{1,0:T(8,128)S(1)} %get-tuple-element.17, ...), kind=kOutput, calls=%fused_computation.5 | convolution fusion | flops 1663352832 | bytes 5111808 | tf_op jit(solution)/shard_map/rd,shkd->shkr/dot_general | solution.py:58
  49.8 0.4 multiply_subtract_fusion.1
  50.2 0.2 pad_maximum_fusion.1
  50.4 0.5 copy-done
  50.9 2.1 %fusion.2 = f32[32,2,16,256]{3,0,2,1:T(8,128)S(1)} fusion(f32[2,66,16,256]{3,2,1,0:T(8,128)S(1)} %pad_maximum_fusion.1, f32[32,33]{1,0:T(8,128)S(1)} %get-tuple-element.19, f32[32,33]{1,0:T(8,128)S(1)} %get-tuple-element.18, f32[66]{0:T(128)S(1)} %copy-done), kind=kOutput, calls=%fused_computation.3 | convolution fusion | flops 103813248 | bytes 3219976 | tf_op jit(solution)/shard_map/ac,sckr->askr/dot_general | solution.py:28
  53.0 0.3 fusion.16
  53.4 0.2 copy.49
  53.6 0.4 fusion.20
  54.1 22.1 %all_to_all.10 = bf16[2,32,16,256]{3,2,0,1:T(8,128)(2,1)S(1)} all-to-all(bf16[2,32,16,256]{3,2,0,1:T(8,128)(2,1)S(1)} %copy.29), channel_id=1, replica_groups=mesh['pipe'=2,'seq'=32,'chan'=4] {'seq'}, dimensions={1} | all-to-all | bytes 1048576 | tf_op jit(solution)/shard_map/all_to_all | solution.py:125
  76.4 4.1 %collective-permute-start = (bf16[1,256,512]{2,1,0:T(8,128)(2,1)S(1)}, bf16[1,256,512]{2,1,0:T(8,128)(2,1)S(1)}, u32[]{:S(2)}, u32[]{:S(2)}) collective-permute-start(bf16[1,256,512]{2,1,0:T(8,128)(2,1)S(1)} %bitcast.56), channel_id=1, source_target_pairs={{128,0},{0,128},{129,1},{1,129},{130,2},{2,130},{131,3},{3,131},{1... | collective-permute-start | bytes 786440 | tf_op jit(solution)/shard_map/ppermute | solution.py:17
  80.5 1.0 %copy.31 = f32[512,256]{0,1:T(8,128)} copy(f32[512,256]{1,0:T(8,128)S(1)} %bitcast_convert_fusion) | data formatting | bytes 1048576 | tf_op jit(solution)/shard_map/broadcast_in_dim | solution.py:130
  81.6 0.7 copy.51
  (16 shorter events, 0.7 us)
Async XLA Ops:
  4.3 36.7 %all-to-all-start = ((bf16[32,4,16,256]{3,2,1,0:T(8,128)(2,1)}), bf16[32,4,16,256]{3,2,1,0:T(8,128)(2,1)S(1)}, u32[]{:S(2)}, u32[]{:S(2)}) async-start(bf16[32,4,16,256]{3,2,1,0:T(8,128)(2,1)} %shard_map.158), calls=%async_computation | async-start | bytes 2097152 | tf_op jit(solution)/shard_map/all_to_all | solution.py:100
  50.2 0.7 copy-start
  76.4 5.3 %collective-permute-start = (bf16[1,256,512]{2,1,0:T(8,128)(2,1)S(1)}, bf16[1,256,512]{2,1,0:T(8,128)(2,1)S(1)}, u32[]{:S(2)}, u32[]{:S(2)}) collective-permute-start(bf16[1,256,512]{2,1,0:T(8,128)(2,1)S(1)} %bitcast.56), channel_id=1, source_target_pairs={{128,0},{0,128},{129,1},{1,129},{130,2},{2,130},{131,3},{3,131},{1... | collective-permute-start | bytes 786440 | tf_op jit(solution)/shard_map/ppermute | solution.py:17

commit v14 on v11

--- a/solution.py
+++ b/solution.py
@@ -62,9 +62,9 @@
     cos_t, sin_t = angle_table(half, np.arange(rows), padded)
     cos_t = cos_t[:, None, :]
     sin_t = sin_t[:, None, :]
-    twisted = jnp.concatenate(
-        [back_real * cos_t - back_imag * sin_t, back_imag * cos_t + back_real * sin_t], axis=1
-    )
+    twisted = jnp.concatenate([back_real, back_imag], axis=1) * jnp.concatenate(
+        [cos_t, cos_t], axis=0
+    ) + jnp.concatenate([back_imag, back_real], axis=1) * jnp.concatenate([-sin_t, sin_t], axis=0)
     weight = np.full(half_count, 2.0)
     weight[0] = 1.0
     weight[blocks] = 1.0

time: 81.5 us -> 81.5 us (level)
  transfers between devices with their start and end apart: 2 -> 2, of which waited for: 2 -> 2; matrix products, arithmetic and copies ran while one was open for 4% -> 5% of each run, Pallas kernels for 0% -> 0%
where the time goes in v14:
time: 81.5 us; the launch traced here: 81.2 us
  waiting for transfers between devices  22.3 us (27%)
  blocking collectives  22.1 us (27%)
  starting transfers between devices  16 us (20%)
  matrix products  9.33 us (11%)
  other arithmetic  4.67 us (6%)
  local copies, waits for them, and re-layouts  3.45 us (4%)
  Pallas kernels  2.58 us (3%)
  between operations  0.86 us (1%)
    all_to_all x1, waiting for transfers between devices, body(): recv = lax.all_to_all(send, 'seq', split_axis=0, concat_axis=0, tiled=True)  22.2 us
    all_to_all x1, blocking collectives, body(): lax.all_to_all(outgoing, 'seq', split_axis=1, concat_axis=1, tiled=True)  22.1 us
    all_to_all x1, starting transfers between devices, body(): recv = lax.all_to_all(send, 'seq', split_axis=0, concat_axis=0, tiled=True)  11.9 us
    dot_general x1, matrix products, forward(): spectrum = jnp.einsum('rd,shkr->shkd', table, twisted, precision=PRECISION)  4.13 us
    ppermute x1, starting transfers between devices, shifted(): return lax.ppermute(block, axis, route)  4.1 us
    dot_general x2, matrix products, contract(): jnp.einsum(form, jnp.asarray(table, jnp.float32), values, precision=PRECI...  3.28 us
    pallas_call x1, Pallas kernels, body(): pl.pallas_call(prep_kernel, out_shape=jax.ShapeDtypeStruct((devices, 4, g...  2.58 us
    dot_general x1, matrix products, inverse(): jnp.einsum('rd,shkd->shkr', table, jnp.concatenate([real, imag], axis=-1)...  1.91 us
  transfers between devices with their start and end apart: 2, of which 2 were waited for; matrix products, arithmetic and copies ran while one was open for 5% of the time, Pallas kernels for 0%

profile of v14, /device:TPU:1, one launch (start us, length us, event | category | flops | bytes accessed | tf_op | source)
XLA Modules:
  0.0 81.2 jit_solution(7799674551232611784)
XLA Ops:
  0.6 2.6 %shard_map.158 = bf16[32,4,16,256]{3,2,1,0:T(8,128)(2,1)} custom-call(bf16[256,512]{1,0:T(8,128)(2,1)} %bitcast.55, bf16[256,512]{1,0:T(8,128)(2,1)} %bitcast.56, bf16[256,512]{1,0:T(8,128)(2,1)} %bitcast.57, bf16[256,512]{1,0:T(8,128)(2,1)} %bitcast.58, bf16[256,512]{1,0:T(8,128)(2,1)} %bitcast.59), custom_call_target="tpu_custom_call" | custom-call | tf_op jit(solution)/shard_map/pallas_call | solution.py:91
  3.2 11.9 %all-to-all-start = ((bf16[32,4,16,256]{3,2,1,0:T(8,128)(2,1)}), bf16[32,4,16,256]{3,2,1,0:T(8,128)(2,1)S(1)}, u32[]{:S(2)}, u32[]{:S(2)}) async-start(bf16[32,4,16,256]{3,2,1,0:T(8,128)(2,1)} %shard_map.158), calls=%async_computation | async-start | bytes 2097152 | tf_op jit(solution)/shard_map/all_to_all | solution.py:94
  15.1 0.8 fusion.65
  15.9 0.2 fusion.39
  16.2 0.2 fusion.63
  16.4 0.2 fusion.41
  16.6 1.1 %fusion.25 = (f32[256,256]{1,0:T(8,128)S(1)}, f32[256,256]{1,0:T(8,128)S(1)}, f32[256,256]{1,0:T(8,128)S(1)}) fusion(s32[256]{0:T(256)S(1)} %iota.6), kind=kLoop, calls=%fused_computation.50 | loop fusion | flops 983040 | bytes 787456 | tf_op jit(solution)/shard_map/neg | solution.py:36
  17.8 22.2 %all-to-all-done = bf16[32,4,16,256]{3,2,1,0:T(8,128)(2,1)S(1)} async-done(((bf16[32,4,16,256]{3,2,1,0:T(8,128)(2,1)}), bf16[32,4,16,256]{3,2,1,0:T(8,128)(2,1)S(1)}, u32[]{:S(2)}, u32[]{:S(2)}) %all-to-all-start) | async-done | bytes 1048608 | tf_op jit(solution)/shard_map/all_to_all | solution.py:94
  40.0 1.2 %convolution_bitcast_fusion = f32[3,66,16,256]{3,1,2,0:T(8,128)S(1)} fusion(bf16[3,32,16,256]{3,2,0,1:T(8,128)(2,1)S(1)} %slice_bitcast_fusion, f32[33,32]{0,1:T(8,128)S(1)} %get-tuple-element.26, f32[33,32]{0,1:T(8,128)S(1)} %get-tuple-element.25), kind=kOutput, calls=%fused_computation.16 | convolution fusion | flops 155715648 | bytes 4038912 | tf_op jit(solution)/shard_map/ja,sakr->sjkr/dot_general | solution.py:28
  41.2 0.5 multiply_add_fusion
  41.8 0.6 pad_maximum_fusion
  42.4 4.1 %fusion = f32[3,33,16,512]{3,2,1,0:T(8,128)S(1)} fusion(f32[3,33,16,512]{3,1,2,0:T(8,128)S(1)} %pad_maximum_fusion, f32[256,256]{1,0:T(8,128)S(1)} %get-tuple-element.17, f32[256,256]{1,0:T(8,128)S(1)} %get-tuple-element.16, f32[256,256]{1,0:T(8,128)S(1)} %get-tuple-element.15), kind=kOutput, calls=%fused_computation.1 | convolution fusion | flops 2492203008 | bytes 7274496 | tf_op jit(solution)/shard_map/rd,shkr->shkd/dot_general | solution.py:50
  46.5 0.3 multiply_add_fusion.2
  46.8 1.9 %fusion.4 = f32[2,33,16,512]{3,2,1,0:T(8,128)S(1)} fusion(f32[1,33,16,256]{3,2,1,0:T(8,128)S(1)} %get-tuple-element.7, f32[1,33,16,256]{3,2,1,0:T(8,128)S(1)} %get-tuple-element.6, f32[1,33,16,256]{3,2,1,0:T(8,128)S(1)} %get-tuple-element.5, f32[1,33,16,256]{3,2,1,0:T(8,128)S(1)} %get-tuple-element.4, f32[256,256]{1,0:T(8,128)S(1)} %get-tuple-element.17, ...), kind=kOutput, calls=%fused_computation.5 | convolution fusion | flops 1663352832 | bytes 5111808 | tf_op jit(solution)/shard_map/rd,shkd->shkr/dot_general | solution.py:58
  48.8 0.3 fusion.71
  49.1 0.5 fusion.12
  49.7 2.1 %fusion.2 = f32[32,2,16,256]{3,0,2,1:T(8,128)S(1)} fusion(f32[2,66,16,256]{3,2,1,0:T(8,128)S(1)} %fusion.12, f32[32,33]{1,0:T(8,128)S(1)} %get-tuple-element.19, f32[32,33]{1,0:T(8,128)S(1)} %get-tuple-element.18, f32[66]{0:T(128)S(1)} %copy-done), kind=kOutput, calls=%fused_computation.3 | convolution fusion | flops 103813248 | bytes 3219976 | tf_op jit(solution)/shard_map/ac,sckr->askr/dot_general | solution.py:28
  51.9 0.3 fusion.17
  52.3 0.2 copy.49
  52.5 0.4 fusion.21
  53.0 22.1 %all_to_all.10 = bf16[2,32,16,256]{3,2,0,1:T(8,128)(2,1)S(1)} all-to-all(bf16[2,32,16,256]{3,2,0,1:T(8,128)(2,1)S(1)} %copy.29), channel_id=1, replica_groups=mesh['pipe'=2,'seq'=32,'chan'=4] {'seq'}, dimensions={1} | all-to-all | bytes 1048576 | tf_op jit(solution)/shard_map/all_to_all | solution.py:119
  75.3 4.1 %collective-permute-start = (bf16[1,256,512]{2,1,0:T(8,128)(2,1)S(1)}, bf16[1,256,512]{2,1,0:T(8,128)(2,1)S(1)}, u32[]{:S(2)}, u32[]{:S(2)}) collective-permute-start(bf16[1,256,512]{2,1,0:T(8,128)(2,1)S(1)} %bitcast.60), channel_id=1, source_target_pairs={{128,0},{0,128},{129,1},{1,129},{130,2},{2,130},{131,3},{3,131},{1... | collective-permute-start | bytes 786440 | tf_op jit(solution)/shard_map/ppermute | solution.py:17
  79.4 1.0 %copy.31 = f32[512,256]{0,1:T(8,128)} copy(f32[512,256]{1,0:T(8,128)S(1)} %bitcast_convert_fusion) | data formatting | bytes 1048576 | tf_op jit(solution)/shard_map/broadcast_in_dim | solution.py:124
  80.5 0.7 copy.51
  (18 shorter events, 0.9 us)
Async XLA Ops:
  3.2 36.7 %all-to-all-start = ((bf16[32,4,16,256]{3,2,1,0:T(8,128)(2,1)}), bf16[32,4,16,256]{3,2,1,0:T(8,128)(2,1)S(1)}, u32[]{:S(2)}, u32[]{:S(2)}) async-start(bf16[32,4,16,256]{3,2,1,0:T(8,128)(2,1)} %shard_map.158), calls=%async_computation | async-start | bytes 2097152 | tf_op jit(solution)/shard_map/all_to_all | solution.py:94
  49.1 0.7 copy-start
  75.3 5.3 %collective-permute-start = (bf16[1,256,512]{2,1,0:T(8,128)(2,1)S(1)}, bf16[1,256,512]{2,1,0:T(8,128)(2,1)S(1)}, u32[]{:S(2)}, u32[]{:S(2)}) collective-permute-start(bf16[1,256,512]{2,1,0:T(8,128)(2,1)S(1)} %bitcast.60), channel_id=1, source_target_pairs={{128,0},{0,128},{129,1},{1,129},{130,2},{2,130},{131,3},{3,131},{1... | collective-permute-start | bytes 786440 | tf_op jit(solution)/shard_map/ppermute | solution.py:17
